TPU v7x, 256 devices: a whole 4x4x8 slice. The times are simulated.
256 devices in a mesh: cfg: 2 (over core), req: 8 (over z), seq: 16 (over y, x).
Axes of the slice: x: 4, y: 4, z: 8, core: 2. Of those that a mesh axis runs over, the one named last changes fastest.
Arguments:
- img_hidden: bfloat16 [2, 16, 512, 1536], P('cfg', 'req', 'seq'), may hold values from -6 to 6
- txt_hidden: bfloat16 [2, 16, 160, 1536], P('cfg', 'req', 'seq'), may hold values from -6 to 6
- text_len: int32 [2, 16], P('cfg'), may hold values from 1 to 154, as said below
- pooled: float32 [2, 16, 1536], P('cfg'), may hold values from -6 to 6
- timestep: int32 [16], replicated, may hold values from 0 to 27
- latent: float32 [16, 512, 64], P('req', 'seq', 'cfg'), may hold values from -24 to 24
- mod_weight: bfloat16 [1536, 15360], P(None, ('req', 'seq')), may hold values from -0.15625 to 0.15625
- mod_bias: float32 [15360], P(('req', 'seq')), may hold values from -2 to 2
- img_qkv: bfloat16 [1536, 3, 1536], P(None, None, 'req'), may hold values from -2.5 to 2.5
- txt_kv: bfloat16 [1536, 2, 1536], P(None, None, 'req'), may hold values from -0.15625 to 0.15625
- out_weight: bfloat16 [1536, 1536], P('req'), may hold values from -0.15625 to 0.15625
- fc_in: bfloat16 [1536, 6144], P(None, 'seq'), may hold values from -0.15625 to 0.15625
- fc_out: bfloat16 [6144, 1536], P('seq'), may hold values from -0.078125 to 0.078125
- final_weight: bfloat16 [1536, 64], replicated, may hold values from -0.15625 to 0.15625
Outputs:
- velocity: float32 [16, 512, 64], P('req', 'seq', 'cfg')
- next_latent: float32 [16, 512, 64], P('req', 'seq', 'cfg')
- latent_norm: float32 [16], P('req')
- latent_peak: float32 [16], P('req')
Inputs may be any that keep to these rules, and one draw needn't show every extreme that they name: Text slots from text_len to 159 of a request are padding; every draw has a request of length 154 and one of length 1.
All inputs are finite; a program needn't handle non-finite values.
Results may differ from a plain program's by a relative error of at most 0.015.
Values may be sent and summed in bfloat16 or wider, within the bound.
No kernel may reach another device: no remote copies, remote signals or barrier semaphores. Data moves between devices by JAX's collectives and lax.ppermute only.
A program may use at most 64 MiB of HBM per device.

v0:
```python
import math

import jax
import jax.numpy as jnp
from jax import lax
from jax.sharding import PartitionSpec as P


D = 1536
HD = 64
PATCHC = 64
IMG = 512
STEPS = 28


SIGMA_SHIFT = 3.0
GUIDANCE = 5.0
EPSILON = 1e-06
MASKED_SCORE = -1e30


def xor_pairs(axis, distance):
    return [(source, source ^ distance) for source in range(lax.axis_size(axis))]


def shifted(fraction):
    return SIGMA_SHIFT * fraction / (1.0 + (SIGMA_SHIFT - 1.0) * fraction)


def plan(timestep):
    position = timestep.astype(jnp.float32)
    return (shifted(1.0 - position / STEPS), shifted(1.0 - (position + 1.0) / STEPS))


def time_features(sigma):
    half_width = D // 2
    frequency = jnp.exp(-math.log(10000.0) * jnp.arange(half_width, dtype=jnp.float32) / half_width)
    angles = (1000.0 * sigma)[:, None] * frequency[None, :]
    return jnp.concatenate([jnp.cos(angles), jnp.sin(angles)], axis=1)


def layer_norm(values):
    average = jnp.mean(values, axis=-1, keepdims=True)
    centred = values - average
    spread = jnp.mean(centred * centred, axis=-1, keepdims=True)
    return centred * lax.rsqrt(spread + EPSILON)


def gather_by_a2a(value, axis):
    count = lax.axis_size(axis)
    copies = jnp.broadcast_to(value[None], (count,) + value.shape)
    return lax.all_to_all(copies, axis, 0, 0, tiled=True)


def ring_gather(value, axis):
    count = lax.axis_size(axis)
    up = [(source, (source + 1) % count) for source in range(count)]
    down = [(source, (source - 1) % count) for source in range(count)]
    ahead = {0: value}
    from_below, from_above = value, value
    for step in range(1, count // 2 + 1):
        from_below = lax.ppermute(from_below, axis, up)
        ahead[count - step] = from_below
        if step < count - step:
            from_above = lax.ppermute(from_above, axis, down)
            ahead[step] = from_above
    return jnp.stack([ahead[k] for k in range(count)])


def attention(queries, key_rows, value_rows, live_keys):
    scale_factor = HD ** (-0.5)
    scores = (
        jnp.einsum("qhd,khd->hqk", queries, key_rows, preferred_element_type=jnp.float32)
        * scale_factor
    )
    scores = jnp.where(live_keys[None, None, :], scores, MASKED_SCORE)
    highest = jnp.max(scores, axis=-1, keepdims=True)
    exp_scores = jnp.exp(scores - highest)
    weights = (exp_scores / jnp.sum(exp_scores, axis=-1, keepdims=True)).astype(jnp.bfloat16)
    mixture = jnp.einsum("hqk,khd->qhd", weights, value_rows, preferred_element_type=jnp.float32)
    return mixture.astype(jnp.bfloat16)


def on_device(
    img_hidden,
    txt_hidden,
    text_len,
    pooled,
    timestep,
    latent,
    mod_weight,
    mod_bias,
    img_qkv,
    txt_kv,
    out_weight,
    fc_in,
    fc_out,
    final_weight,
):
    group_size = img_hidden.shape[1]
    req_count = lax.axis_size("req")
    seq_count = lax.axis_size("seq")
    half_index = lax.axis_index("cfg")
    cond_first = half_index == 0
    split_rows = out_weight.shape[0] // 2
    own_part = lax.dynamic_slice_in_dim(out_weight, half_index * split_rows, split_rows, 0)
    gathered_part = ring_gather(own_part, "req")
    partner_part = lax.ppermute(gathered_part, "cfg", xor_pairs("cfg", 1))
    every_weight = jnp.concatenate(
        [
            jnp.where(cond_first, gathered_part, partner_part),
            jnp.where(cond_first, partner_part, gathered_part),
        ],
        axis=1,
    )
    half_values = latent.shape[2]
    partner_latent = lax.ppermute(latent, "cfg", xor_pairs("cfg", 1))
    full_latent = jnp.concatenate(
        [
            jnp.where(cond_first, latent, partner_latent),
            jnp.where(cond_first, partner_latent, latent),
        ],
        axis=2,
    )
    current, upcoming = plan(timestep)
    activated = jax.nn.silu(pooled[0] + time_features(current)).astype(jnp.bfloat16)
    columns = jnp.dot(activated, mod_weight, preferred_element_type=jnp.float32) + mod_bias
    block_width = columns.shape[1]
    mine = lax.all_to_all(
        columns.reshape(req_count, group_size, block_width), "req", 0, 0, tiled=True
    )
    every = gather_by_a2a(mine, "seq")
    every = every.transpose(2, 1, 0, 3).reshape(group_size, req_count * seq_count * block_width)
    modulation = every.reshape(group_size, 10, 1, D)
    shift_attn, scale_attn, gate_attn = (modulation[:, 0], modulation[:, 1], modulation[:, 2])
    shift_mlp, scale_mlp, gate_mlp = (modulation[:, 3], modulation[:, 4], modulation[:, 5])
    shift_text, scale_text = (modulation[:, 6], modulation[:, 7])
    scale_final, shift_final = (modulation[:, 8], modulation[:, 9])
    img_float = img_hidden[0].astype(jnp.float32)
    img_in = (layer_norm(img_float) * (1.0 + scale_attn) + shift_attn).astype(jnp.bfloat16)
    txt_in = (
        layer_norm(txt_hidden[0].astype(jnp.float32)) * (1.0 + scale_text) + shift_text
    ).astype(jnp.bfloat16)
    row_count = img_in.shape[1]
    text_block = txt_in.shape[1]
    both = ring_gather(jnp.concatenate([img_in, txt_in], axis=1), "req")
    both = both.reshape(req_count * group_size, row_count + text_block, D)
    head_width = img_qkv.shape[2]
    local_heads = head_width // HD
    qkv_columns = img_qkv.reshape(D, 3 * head_width)
    kv_columns = txt_kv.reshape(D, 2 * head_width)
    proj_img = jnp.einsum(
        "rnd,dc->rnc", both[:, :row_count], qkv_columns, preferred_element_type=jnp.float32
    ).astype(jnp.bfloat16)
    proj_txt = jnp.einsum(
        "rnd,dc->rnc", both[:, row_count:], kv_columns, preferred_element_type=jnp.float32
    ).astype(jnp.bfloat16)
    request_count = proj_img.shape[0]
    img_size = row_count * 3 * head_width
    packed = jnp.concatenate(
        [proj_img.reshape(request_count, img_size), proj_txt.reshape(request_count, -1)], axis=1
    )
    packed = jnp.roll(packed, lax.axis_index("req") * group_size, axis=0)
    own = lax.all_to_all(packed, "seq", 0, 0, tiled=True)
    image_rows = seq_count * row_count
    text_rows = seq_count * text_block
    own_img = own[:, :img_size].reshape(image_rows, 3 * head_width)
    own_txt = own[:, img_size:].reshape(text_rows, 2 * head_width)
    queries = own_img[:, :head_width]
    key_rows = jnp.concatenate([own_img[:, head_width : 2 * head_width], own_txt[:, :head_width]], 0)
    value_rows = jnp.concatenate([own_img[:, 2 * head_width :], own_txt[:, head_width:]], 0)
    text_count = lax.dynamic_index_in_dim(text_len[0], lax.axis_index("seq"), 0, False)
    total_keys = image_rows + text_rows
    live_keys = jnp.arange(total_keys, dtype=jnp.int32) < image_rows + text_count
    attended = attention(
        queries.reshape(image_rows, local_heads, HD),
        key_rows.reshape(total_keys, local_heads, HD),
        value_rows.reshape(total_keys, local_heads, HD),
        live_keys,
    ).reshape(seq_count, row_count, head_width)
    attended_rows = lax.all_to_all(attended, "seq", 0, 0, tiled=True)
    head_columns = lax.all_to_all(
        attended_rows.reshape(req_count, group_size, row_count, head_width), "req", 0, 0, tiled=True
    )
    head_columns = jnp.roll(head_columns, -lax.axis_index("req"), axis=0)
    attn_out = jnp.einsum(
        "grnk,gkd->rnd", head_columns, every_weight, preferred_element_type=jnp.float32
    )
    img_mid = img_float + gate_attn * attn_out
    mlp_in = (layer_norm(img_mid) * (1.0 + scale_mlp) + shift_mlp).astype(jnp.bfloat16)
    all_rows = gather_by_a2a(mlp_in, "seq")
    raised = jnp.einsum("srnd,df->srnf", all_rows, fc_in, preferred_element_type=jnp.float32)
    hidden = jax.nn.gelu(raised, approximate=True).astype(jnp.bfloat16)
    mlp_terms = jnp.einsum(
        "srnf,fd->srnd", hidden, fc_out, preferred_element_type=jnp.float32
    ).astype(jnp.bfloat16)
    block_terms = lax.all_to_all(mlp_terms, "seq", 0, 0, tiled=True)
    mlp_out = jnp.sum(block_terms.astype(jnp.float32), axis=0)
    img_out = img_mid + gate_mlp * mlp_out
    final_in = (layer_norm(img_out) * (1.0 + scale_final) + shift_final).astype(jnp.bfloat16)
    own_velocity = jnp.einsum(
        "rnd,dc->rnc", final_in, final_weight, preferred_element_type=jnp.float32
    )
    other_velocity = lax.ppermute(own_velocity, "cfg", xor_pairs("cfg", 1))
    conditional = jnp.where(cond_first, own_velocity, other_velocity)
    unconditional = jnp.where(cond_first, other_velocity, own_velocity)
    guided = unconditional + GUIDANCE * (conditional - unconditional)
    offset = lax.axis_index("req") * group_size
    step_size = lax.dynamic_slice_in_dim(upcoming - current, offset, group_size, 0)
    next_latent = full_latent + step_size[:, None, None] * guided
    squares = jnp.sum(next_latent * next_latent, axis=(1, 2))
    largest = jnp.max(jnp.abs(next_latent), axis=(1, 2))
    distance = 1
    while distance < seq_count:
        stats = lax.ppermute(jnp.stack([squares, largest]), "seq", xor_pairs("seq", distance))
        squares = squares + stats[0]
        largest = jnp.maximum(largest, stats[1])
        distance *= 2
    guided = lax.dynamic_slice_in_dim(guided, half_index * half_values, half_values, 2)
    next_latent = lax.dynamic_slice_in_dim(next_latent, half_index * half_values, half_values, 2)
    latent_norm = jnp.sqrt(squares / (IMG * PATCHC))
    return (guided, next_latent, latent_norm, largest)


def solution(mesh):
    placed = (
        P("cfg", "req", "seq", None),
        P("cfg", "req", "seq", None),
        P("cfg", None),
        P("cfg", None, None),
        P(),
        P("req", "seq", "cfg"),
        P(None, ("req", "seq")),
        P(("req", "seq")),
        P(None, None, "req"),
        P(None, None, "req"),
        P("req", None),
        P(None, "seq"),
        P("seq", None),
        P(),
    )
    return jax.shard_map(
        on_device,
        mesh=mesh,
        in_specs=placed,
        out_specs=(P("req", "seq", "cfg"), P("req", "seq", "cfg"), P("req"), P("req")),
        check_vma=False,
    )
```

profile of v0, /device:TPU:1, one launch (start us, length us, event | category | flops | bytes accessed | tf_op | source)
XLA Modules:
  0.0 268.7 jit_solution(11631216505841354597)
XLA Ops:
  0.7 1.9 bitcast_dynamic-update-slice_fusion.7
  2.5 6.4 %collective-permute-start.7 = (bf16[96,1536]{1,0:T(8,128)(2,1)S(1)}, bf16[96,1536]{1,0:T(8,128)(2,1)S(1)}, u32[]{:S(2)}, u32[]{:S(2)}) collective-permute-start(bf16[96,1536]{1,0:T(8,128)(2,1)S(1)} %get-tuple-element.13), channel_id=1, source_target_pairs={{0,112},{16,0},{32,16},{48,32},{64,48},{80,64},{96,80},{112,96},{1... | collective-permute-start | bytes 884744 | tf_op jit(solution)/shard_map/ppermute | solution.py:65
  9.9 1.8 convolution_add_fusion
  11.7 4.1 %all-to-all-start = ((f32[8,2,120]{2,1,0:T(2,128)}), f32[8,2,120]{2,1,0:T(2,128)S(1)}, u32[]{:S(2)}, u32[]{:S(2)}) async-start(f32[8,2,120]{2,1,0:T(2,128)} %bitcast.2), calls=%async_computation | async-start | bytes 16384 | tf_op jit(solution)/shard_map/all_to_all | solution.py:129
  16.8 1.1 fusion.53
  19.9 2.5 all-to-all-done
  23.0 6.8 %all-to-all-start.1 = ((f32[16,8,2,120]{3,1,2,0:T(8,128)}), f32[16,8,2,120]{3,1,2,0:T(8,128)S(1)}, u32[]{:S(2)}, u32[]{:S(2)}) async-start(f32[16,8,2,120]{3,1,2,0:T(8,128)} %broadcast_in_dim.12), calls=%async_computation.1 | async-start | bytes 262144 | tf_op jit(solution)/shard_map/all_to_all | solution.py:52
  29.8 6.8 %all-to-all-done.1 = f32[16,8,2,120]{3,1,2,0:T(8,128)S(1)} async-done(((f32[16,8,2,120]{3,1,2,0:T(8,128)}), f32[16,8,2,120]{3,1,2,0:T(8,128)S(1)}, u32[]{:S(2)}, u32[]{:S(2)}) %all-to-all-start.1) | async-done | bytes 122912 | tf_op jit(solution)/shard_map/all_to_all | solution.py:52
  37.6 1.2 collective-permute-start.3
  38.9 1.6 collective-permute-start.8
  41.2 1.7 collective-permute-done
  42.9 1.5 collective-permute-start.1
  44.4 3.7 %collective-permute-done.8 = bf16[96,1536]{1,0:T(8,128)(2,1)S(1)} collective-permute-done((bf16[96,1536]{1,0:T(8,128)(2,1)S(1)}, bf16[96,1536]{1,0:T(8,128)(2,1)S(1)}, u32[]{:S(2)}, u32[]{:S(2)}) %collective-permute-start.8) | collective-permute-done | bytes 294944 | tf_op jit(solution)/shard_map/ppermute | solution.py:65
  48.2 1.5 collective-permute-start.9
  50.4 4.1 %collective-permute-done.1 = bf16[2,42,1536]{2,1,0:T(8,128)(2,1)S(1)} collective-permute-done((bf16[2,42,1536]{2,1,0:T(8,128)(2,1)S(1)}, bf16[2,42,1536]{2,1,0:T(8,128)(2,1)S(1)}, u32[]{:S(2)}, u32[]{:S(2)}) %collective-permute-start.1) | collective-permute-done | bytes 258080 | tf_op jit(solution)/shard_map/ppermute | solution.py:65
  54.5 1.5 collective-permute-start.2
  56.0 6.0 %collective-permute-done.12 = bf16[96,1536]{1,0:T(8,128)(2,1)} collective-permute-done((bf16[96,1536]{1,0:T(8,128)(2,1)S(1)}, bf16[96,1536]{1,0:T(8,128)(2,1)}, u32[]{:S(2)}, u32[]{:S(2)}) %collective-permute-start.12) | collective-permute-done | bytes 294944 | tf_op jit(solution)/shard_map/ppermute | solution.py:62
  62.7 5.7 %collective-permute-done.5 = bf16[2,42,1536]{2,1,0:T(8,128)(2,1)S(1)} collective-permute-done((bf16[2,42,1536]{2,1,0:T(8,128)(2,1)S(1)}, bf16[2,42,1536]{2,1,0:T(8,128)(2,1)S(1)}, u32[]{:S(2)}, u32[]{:S(2)}) %collective-permute-start.5) | collective-permute-done | bytes 258080 | tf_op jit(solution)/shard_map/ppermute | solution.py:62
  68.4 12.6 %collective-permute-done.6 = bf16[2,42,1536]{2,1,0:T(8,128)(2,1)S(1)} collective-permute-done((bf16[2,42,1536]{2,1,0:T(8,128)(2,1)S(1)}, bf16[2,42,1536]{2,1,0:T(8,128)(2,1)S(1)}, u32[]{:S(2)}, u32[]{:S(2)}) %collective-permute-start.6) | collective-permute-done | bytes 258080 | tf_op jit(solution)/shard_map/ppermute | solution.py:62
  81.2 1.4 copy-done.8
  82.6 1.4 fusion.30
  84.8 2.1 convolution_convert_fusion.1
  87.0 3.2 %fusion.46 = bf16[16,1,22272]{2,0,1:T(8,128)(2,1)S(1)} fusion(s32[]{:T(128)S(6)} %select_n.79, bf16[16,18432]{1,0:T(8,128)(2,1)S(1)} %reshape.170, bf16[16,3840]{1,0:T(8,128)(2,1)S(1)} %bitcast.204), kind=kLoop, calls=%fused_computation.50 | loop fusion | flops 2850816 | bytes 1425412 | tf_op jit(solution)/shard_map/all_to_all | solution.py:164
  90.7 1.2 reduce.2
  91.9 1.1 reshape.187
  93.0 4.3 %all-to-all-start.2 = ((bf16[16,2,11136]{2,1,0:T(2,128)(2,1)}), bf16[16,2,11136]{2,1,0:T(2,128)(2,1)}, u32[]{:S(2)}, u32[]{:S(2)}) async-start(bf16[16,2,11136]{2,1,0:T(2,128)(2,1)} %reshape.187), calls=%async_computation.2 | async-start | bytes 1425408 | tf_op jit(solution)/shard_map/all_to_all | solution.py:164
  97.3 1.7 bitcast_dynamic-update-slice_fusion.3
  99.0 1.7 bitcast_dynamic-update-slice_fusion.2
  102.2 5.3 %collective-permute-start.14 = (bf16[8,96,1536]{2,1,0:T(8,128)(2,1)}, bf16[8,96,1536]{2,1,0:T(8,128)(2,1)}, u32[]{:S(2)}, u32[]{:S(2)}) collective-permute-start(bf16[8,96,1536]{2,1,0:T(8,128)(2,1)} %bitcast_dynamic-update-slice_fusion), channel_id=1, source_target_pairs={{0,128},{128,0},{1,129},{129,1},{2,130},{130,2},{3,131},{131,3},{4... | collective-permute-start | bytes 7077896 | tf_op jit(solution)/shard_map/ppermute | solution.py:108
  108.7 4.2 %reshape.188 = bf16[16,1,22272]{2,1,0:T(2,128)(2,1)S(1)} reshape(bf16[16,2,11136]{2,1,0:T(2,128)(2,1)} %all-to-all-done.2) | data formatting | bytes 1425408
  115.5 4.5 %fusion.89 = (f32[3,512]{1,0:T(4,128)S(1)}, f32[3,512,672]{1,2,0:T(8,128)}) fusion(pred[672]{0:T(1024)(128)(4,1)S(1)} %iota_compare_fusion, bf16[512,3,64]{0,2,1:T(8,128)(2,1)} %bitcast.207, bf16[672,3,64]{0,2,1:T(8,128)(2,1)S(1)} %bitcast.205), kind=kOutput, calls=%fused_computation.181 | convolution fusion | flops 136250016 | bytes 4590240 | tf_op jit(solution)/shard_map/sub | solution.py:78
  120.0 2.7 fusion.36
  124.0 6.9 %all-to-all-start.3 = ((bf16[16,32,192]{2,1,0:T(8,128)(2,1)}), bf16[16,32,192]{2,1,0:T(8,128)(2,1)}, u32[]{:S(2)}, u32[]{:S(2)}) async-start(bf16[16,32,192]{2,1,0:T(8,128)(2,1)} %reshape.178), calls=%async_computation.3 | async-start | bytes 524288 | tf_op jit(solution)/shard_map/all_to_all | solution.py:181
  130.9 7.6 %all-to-all-done.3 = bf16[16,32,192]{2,1,0:T(8,128)(2,1)} async-done(((bf16[16,32,192]{2,1,0:T(8,128)(2,1)}), bf16[16,32,192]{2,1,0:T(8,128)(2,1)}, u32[]{:S(2)}, u32[]{:S(2)}) %all-to-all-start.3) | async-done | bytes 196640 | tf_op jit(solution)/shard_map/all_to_all | solution.py:181
  138.4 4.1 %all-to-all-start.4 = ((bf16[8,2,32,192]{3,2,1,0:T(8,128)(2,1)}), bf16[8,2,32,192]{3,2,1,0:T(8,128)(2,1)S(1)}, u32[]{:S(2)}, u32[]{:S(2)}) async-start(bf16[8,2,32,192]{3,2,1,0:T(8,128)(2,1)} %bitcast.24), calls=%async_computation.4 | async-start | bytes 524288 | tf_op jit(solution)/shard_map/all_to_all | solution.py:182
  142.5 4.8 %broadcast_select_fusion.1 = (bf16[8,96,1536]{2,1,0:T(8,128)(2,1)}, bf16[8,96,1536]{2,1,0:T(8,128)(2,1)}) fusion(bf16[8,96,1536]{2,1,0:T(8,128)(2,1)} %bitcast_dynamic-update-slice_fusion, bf16[8,96,1536]{2,1,0:T(8,128)(2,1)} %collective-permute-done.14, pred[]{:T(512)S(6)} %eq.8), kind=kLoop, calls=%fused_computation.14 | loop fusion | flops 2359296 | bytes 9437185 | tf_op jit(solution)/shard_map/jit(_where)/select_n | solution.py:111
  147.4 4.6 %all-to-all-done.4 = bf16[8,2,32,192]{3,2,1,0:T(8,128)(2,1)S(1)} async-done(((bf16[8,2,32,192]{3,2,1,0:T(8,128)(2,1)}), bf16[8,2,32,192]{3,2,1,0:T(8,128)(2,1)S(1)}, u32[]{:S(2)}, u32[]{:S(2)}) %all-to-all-start.4) | async-done | bytes 196640 | tf_op jit(solution)/shard_map/all_to_all | solution.py:182
  152.0 3.4 %fusion.90 = (f32[2,32]{1,0:T(2,128)S(1)}, f32[2,32,1536]{2,1,0:T(8,128)S(1)}) fusion(bf16[8,96,1536]{2,1,0:T(8,128)(2,1)} %get-tuple-element.15, bf16[8,96,1536]{2,1,0:T(8,128)(2,1)} %get-tuple-element.14, s32[]{:T(128)S(6)} %select_n.83, bf16[8,2,32,192]{3,2,1,0:T(8,128)(2,1)S(1)} %all-to-all-done.4, f32[2,1536]{1,0:T(2,128)S(1)} %bitcast.212, ...), kind=kOutput, calls=%fused_computation.182 | convolution fusion | flops 311918528 | bytes 5517572 | tf_op jit(solution)/shard_map/grnk,gkd->rnd/dot_general | solution.py:186
  156.2 38.9 %all_to_all.42 = bf16[16,2,32,1536]{3,2,1,0:T(8,128)(2,1)} all-to-all(bf16[16,2,32,1536]{3,2,1,0:T(8,128)(2,1)S(1)} %broadcast_in_dim.15), channel_id=1, replica_groups=mesh['cfg'=2,'req'=8,'seq'=16] {'seq'}, dimensions={0} | all-to-all | bytes 6291456 | tf_op jit(solution)/shard_map/all_to_all | solution.py:52
  195.1 7.5 %convolution_convert_fusion = bf16[16,2,32,1536]{3,2,1,0:T(8,128)(2,1)} fusion(bf16[384,1536]{1,0:T(8,128)(2,1)S(1)} %copy-done.10, bf16[16,2,32,1536]{3,2,1,0:T(8,128)(2,1)} %all_to_all.42, bf16[1536,384]{1,0:T(8,128)(2,1)} %param.25), kind=kOutput, calls=%fused_computation.10 | convolution fusion | flops 2421030912 | bytes 8650752 | tf_op jit(solution)/shard_map/srnf,fd->srnd/dot_general | solution.py:194
  202.6 4.6 %all-to-all-start.6 = ((bf16[16,2,32,1536]{3,2,1,0:T(8,128)(2,1)}), bf16[16,2,32,1536]{3,2,1,0:T(8,128)(2,1)}, u32[]{:S(2)}, u32[]{:S(2)}) async-start(bf16[16,2,32,1536]{3,2,1,0:T(8,128)(2,1)} %convolution_convert_fusion), calls=%async_computation.6 | async-start | bytes 6291456 | tf_op jit(solution)/shard_map/all_to_all | solution.py:197
  207.2 5.5 %collective-permute-start.16 = (f32[2,32,32]{2,1,0:T(8,128)S(1)}, f32[2,32,32]{2,1,0:T(8,128)S(1)}, u32[]{:S(2)}, u32[]{:S(2)}) collective-permute-start(f32[2,32,32]{2,1,0:T(8,128)S(1)} %copy-done.9), channel_id=1, source_target_pairs={{0,128},{128,0},{1,129},{129,1},{2,130},{130,2},{3,131},{131,3},{4... | collective-permute-start | bytes 24584 | tf_op jit(solution)/shard_map/ppermute | solution.py:117
  212.8 30.1 %all-to-all-done.6 = bf16[16,2,32,1536]{3,2,1,0:T(8,128)(2,1)} async-done(((bf16[16,2,32,1536]{3,2,1,0:T(8,128)(2,1)}), bf16[16,2,32,1536]{3,2,1,0:T(8,128)(2,1)}, u32[]{:S(2)}, u32[]{:S(2)}) %all-to-all-start.6) | async-done | bytes 3145760 | tf_op jit(solution)/shard_map/all_to_all | solution.py:197
  242.9 2.4 convert_reduce_fusion
  245.9 8.1 %collective-permute-start.15 = (f32[2,32,64]{2,1,0:T(8,128)S(1)}, f32[2,32,64]{2,1,0:T(8,128)S(1)}, u32[]{:S(2)}, u32[]{:S(2)}) collective-permute-start(f32[2,32,64]{2,1,0:T(8,128)S(1)} %fusion.66), channel_id=1, source_target_pairs={{0,128},{128,0},{1,129},{129,1},{2,130},{130,2},{3,131},{131,3},{4... | collective-permute-start | bytes 49160 | tf_op jit(solution)/shard_map/ppermute | solution.py:204
  257.7 3.9 %collective-permute-done.18 = f32[2,2]{1,0:T(2,128)S(1)} collective-permute-done((f32[2,2]{1,0:T(2,128)S(1)}, f32[2,2]{1,0:T(2,128)S(1)}, u32[]{:S(2)}, u32[]{:S(2)}) %collective-permute-start.18) | collective-permute-done | bytes 48 | tf_op jit(solution)/shard_map/ppermute | solution.py:215
  261.7 2.4 collective-permute-done.19
  264.8 3.4 %collective-permute-done.20 = f32[2,2]{1,0:T(2,128)S(1)} collective-permute-done((f32[2,2]{1,0:T(2,128)S(1)}, f32[2,2]{1,0:T(2,128)S(1)}, u32[]{:S(2)}, u32[]{:S(2)}) %collective-permute-start.20) | collective-permute-done | bytes 48 | tf_op jit(solution)/shard_map/ppermute | solution.py:215
  (128 shorter events, 22.5 us)
Async XLA Ops:
  0.6 80.6 %copy-start = (bf16[1536,3,192]{0,2,1:T(8,128)(2,1)S(1)}, bf16[1536,3,192]{0,2,1:T(8,128)(2,1)}, u32[]{:S(2)}) copy-start(bf16[1536,3,192]{0,2,1:T(8,128)(2,1)} %param.22) | copy-start | bytes 5308420
  0.6 36.3 %copy-start.1 = (bf16[1,2,32,1536]{3,2,1,0:T(8,128)(2,1)S(1)}, bf16[1,2,32,1536]{3,2,1,0:T(8,128)(2,1)}, u32[]{:S(2)}) copy-start(bf16[1,2,32,1536]{3,2,1,0:T(8,128)(2,1)} %param.14) | copy-start | bytes 589828
  0.7 36.5 %copy-start.2 = (bf16[1,2,10,1536]{3,1,2,0:T(2,128)(2,1)S(1)}, bf16[1,2,10,1536]{3,1,2,0:T(2,128)(2,1)}, u32[]{:S(2)}) copy-start(bf16[1,2,10,1536]{3,1,2,0:T(2,128)(2,1)} %param.15) | copy-start | bytes 184324
  2.5 36.3 %collective-permute-start.7 = (bf16[96,1536]{1,0:T(8,128)(2,1)S(1)}, bf16[96,1536]{1,0:T(8,128)(2,1)S(1)}, u32[]{:S(2)}, u32[]{:S(2)}) collective-permute-start(bf16[96,1536]{1,0:T(8,128)(2,1)S(1)} %get-tuple-element.13), channel_id=1, source_target_pairs={{0,112},{16,0},{32,16},{48,32},{64,48},{80,64},{96,80},{112,96},{1... | collective-permute-start | bytes 884744 | tf_op jit(solution)/shard_map/ppermute | solution.py:65
  8.9 31.5 %collective-permute-start.10 = (bf16[96,1536]{1,0:T(8,128)(2,1)S(1)}, bf16[96,1536]{1,0:T(8,128)(2,1)S(1)}, u32[]{:S(2)}, u32[]{:S(2)}) collective-permute-start(bf16[96,1536]{1,0:T(8,128)(2,1)S(1)} %get-tuple-element.13), channel_id=1, source_target_pairs={{0,16},{16,32},{32,48},{48,64},{64,80},{80,96},{96,112},{112,0},{1... | collective-permute-start | bytes 884744 | tf_op jit(solution)/shard_map/ppermute | solution.py:62
  11.7 10.7 %all-to-all-start = ((f32[8,2,120]{2,1,0:T(2,128)}), f32[8,2,120]{2,1,0:T(2,128)S(1)}, u32[]{:S(2)}, u32[]{:S(2)}) async-start(f32[8,2,120]{2,1,0:T(2,128)} %bitcast.2), calls=%async_computation | async-start | bytes 16384 | tf_op jit(solution)/shard_map/all_to_all | solution.py:129
  23.0 13.6 %all-to-all-start.1 = ((f32[16,8,2,120]{3,1,2,0:T(8,128)}), f32[16,8,2,120]{3,1,2,0:T(8,128)S(1)}, u32[]{:S(2)}, u32[]{:S(2)}) async-start(f32[16,8,2,120]{3,1,2,0:T(8,128)} %broadcast_in_dim.12), calls=%async_computation.1 | async-start | bytes 262144 | tf_op jit(solution)/shard_map/all_to_all | solution.py:52
  37.3 5.7 %collective-permute-start = (bf16[2,42,1536]{2,1,0:T(8,128)(2,1)S(1)}, bf16[2,42,1536]{2,1,0:T(8,128)(2,1)S(1)}, u32[]{:S(2)}, u32[]{:S(2)}) collective-permute-start(bf16[2,42,1536]{2,1,0:T(8,128)(2,1)S(1)} %pad_maximum_fusion.2), channel_id=1, source_target_pairs={{0,112},{16,0},{32,16},{48,32},{64,48},{80,64},{96,80},{112,96},{1... | collective-permute-start | bytes 774152 | tf_op jit(solution)/shard_map/ppermute | solution.py:65
  37.6 6.8 %collective-permute-start.3 = (bf16[2,42,1536]{2,1,0:T(8,128)(2,1)S(1)}, bf16[2,42,1536]{2,1,0:T(8,128)(2,1)S(1)}, u32[]{:S(2)}, u32[]{:S(2)}) collective-permute-start(bf16[2,42,1536]{2,1,0:T(8,128)(2,1)S(1)} %pad_maximum_fusion.2), channel_id=1, source_target_pairs={{0,16},{16,32},{32,48},{48,64},{64,80},{80,96},{96,112},{112,0},{1... | collective-permute-start | bytes 774152 | tf_op jit(solution)/shard_map/ppermute | solution.py:62
  38.9 9.3 %collective-permute-start.8 = (bf16[96,1536]{1,0:T(8,128)(2,1)S(1)}, bf16[96,1536]{1,0:T(8,128)(2,1)S(1)}, u32[]{:S(2)}, u32[]{:S(2)}) collective-permute-start(bf16[96,1536]{1,0:T(8,128)(2,1)S(1)} %collective-permute-done.7), channel_id=1, source_target_pairs={{0,112},{16,0},{32,16},{48,32},{64,48},{80,64},{96,80},{112,96},{1... | collective-permute-start | bytes 884744 | tf_op jit(solution)/shard_map/ppermute | solution.py:65
  40.4 40.7 %copy-start.3 = (bf16[96,1536]{1,0:T(8,128)(2,1)}, bf16[96,1536]{1,0:T(8,128)(2,1)S(1)}, u32[]{:S(2)}) copy-start(bf16[96,1536]{1,0:T(8,128)(2,1)S(1)} %collective-permute-done.10) | copy-start | bytes 884740
  40.4 9.2 %collective-permute-start.11 = (bf16[96,1536]{1,0:T(8,128)(2,1)S(1)}, bf16[96,1536]{1,0:T(8,128)(2,1)S(1)}, u32[]{:S(2)}, u32[]{:S(2)}) collective-permute-start(bf16[96,1536]{1,0:T(8,128)(2,1)S(1)} %collective-permute-done.10), channel_id=1, source_target_pairs={{0,16},{16,32},{32,48},{48,64},{64,80},{80,96},{96,112},{112,0},{1... | collective-permute-start | bytes 884744 | tf_op jit(solution)/shard_map/ppermute | solution.py:62
  42.9 11.5 %collective-permute-start.1 = (bf16[2,42,1536]{2,1,0:T(8,128)(2,1)S(1)}, bf16[2,42,1536]{2,1,0:T(8,128)(2,1)S(1)}, u32[]{:S(2)}, u32[]{:S(2)}) collective-permute-start(bf16[2,42,1536]{2,1,0:T(8,128)(2,1)S(1)} %collective-permute-done), channel_id=1, source_target_pairs={{0,112},{16,0},{32,16},{48,32},{64,48},{80,64},{96,80},{112,96},{1... | collective-permute-start | bytes 774152 | tf_op jit(solution)/shard_map/ppermute | solution.py:65
  44.4 11.5 %collective-permute-start.4 = (bf16[2,42,1536]{2,1,0:T(8,128)(2,1)S(1)}, bf16[2,42,1536]{2,1,0:T(8,128)(2,1)S(1)}, u32[]{:S(2)}, u32[]{:S(2)}) collective-permute-start(bf16[2,42,1536]{2,1,0:T(8,128)(2,1)S(1)} %collective-permute-done.3), channel_id=1, source_target_pairs={{0,16},{16,32},{32,48},{48,64},{64,80},{80,96},{96,112},{112,0},{1... | collective-permute-start | bytes 774152 | tf_op jit(solution)/shard_map/ppermute | solution.py:62
  48.2 13.8 %collective-permute-start.9 = (bf16[96,1536]{1,0:T(8,128)(2,1)S(1)}, bf16[96,1536]{1,0:T(8,128)(2,1)S(1)}, u32[]{:S(2)}, u32[]{:S(2)}) collective-permute-start(bf16[96,1536]{1,0:T(8,128)(2,1)S(1)} %collective-permute-done.8), channel_id=1, source_target_pairs={{0,112},{16,0},{32,16},{48,32},{64,48},{80,64},{96,80},{112,96},{1... | collective-permute-start | bytes 884744 | tf_op jit(solution)/shard_map/ppermute | solution.py:65
  49.6 31.5 %copy-start.5 = (bf16[96,1536]{1,0:T(8,128)(2,1)}, bf16[96,1536]{1,0:T(8,128)(2,1)S(1)}, u32[]{:S(2)}) copy-start(bf16[96,1536]{1,0:T(8,128)(2,1)S(1)} %collective-permute-done.11) | copy-start | bytes 884740
  49.6 12.4 %collective-permute-start.12 = (bf16[96,1536]{1,0:T(8,128)(2,1)S(1)}, bf16[96,1536]{1,0:T(8,128)(2,1)}, u32[]{:S(2)}, u32[]{:S(2)}) collective-permute-start(bf16[96,1536]{1,0:T(8,128)(2,1)S(1)} %collective-permute-done.11), channel_id=1, source_target_pairs={{0,16},{16,32},{32,48},{48,64},{64,80},{80,96},{96,112},{112,0},{1... | collective-permute-start | bytes 884744 | tf_op jit(solution)/shard_map/ppermute | solution.py:62
  54.5 14.0 %collective-permute-start.2 = (bf16[2,42,1536]{2,1,0:T(8,128)(2,1)S(1)}, bf16[2,42,1536]{2,1,0:T(8,128)(2,1)S(1)}, u32[]{:S(2)}, u32[]{:S(2)}) collective-permute-start(bf16[2,42,1536]{2,1,0:T(8,128)(2,1)S(1)} %collective-permute-done.1), channel_id=1, source_target_pairs={{0,112},{16,0},{32,16},{48,32},{64,48},{80,64},{96,80},{112,96},{1... | collective-permute-start | bytes 774152 | tf_op jit(solution)/shard_map/ppermute | solution.py:65
  56.0 12.5 %collective-permute-start.5 = (bf16[2,42,1536]{2,1,0:T(8,128)(2,1)S(1)}, bf16[2,42,1536]{2,1,0:T(8,128)(2,1)S(1)}, u32[]{:S(2)}, u32[]{:S(2)}) collective-permute-start(bf16[2,42,1536]{2,1,0:T(8,128)(2,1)S(1)} %collective-permute-done.4), channel_id=1, source_target_pairs={{0,16},{16,32},{32,48},{48,64},{64,80},{80,96},{96,112},{112,0},{1... | collective-permute-start | bytes 774152 | tf_op jit(solution)/shard_map/ppermute | solution.py:62
  62.0 35.3 %collective-permute-start.13 = (bf16[96,1536]{1,0:T(8,128)(2,1)}, bf16[96,1536]{1,0:T(8,128)(2,1)}, u32[]{:S(2)}, u32[]{:S(2)}) collective-permute-start(bf16[96,1536]{1,0:T(8,128)(2,1)} %collective-permute-done.12), channel_id=1, source_target_pairs={{0,16},{16,32},{32,48},{48,64},{64,80},{80,96},{96,112},{112,0},{1... | collective-permute-start | bytes 884744 | tf_op jit(solution)/shard_map/ppermute | solution.py:62
  68.4 12.6 %collective-permute-start.6 = (bf16[2,42,1536]{2,1,0:T(8,128)(2,1)S(1)}, bf16[2,42,1536]{2,1,0:T(8,128)(2,1)S(1)}, u32[]{:S(2)}, u32[]{:S(2)}) collective-permute-start(bf16[2,42,1536]{2,1,0:T(8,128)(2,1)S(1)} %collective-permute-done.5), channel_id=1, source_target_pairs={{0,16},{16,32},{32,48},{48,64},{64,80},{80,96},{96,112},{112,0},{1... | collective-permute-start | bytes 774152 | tf_op jit(solution)/shard_map/ppermute | solution.py:62
  81.2 1.4 copy-start.8
  91.9 8.8 %copy-start.6 = (bf16[96,1536]{1,0:T(8,128)(2,1)S(1)}, bf16[96,1536]{1,0:T(8,128)(2,1)}, u32[]{:S(2)}) copy-start(bf16[96,1536]{1,0:T(8,128)(2,1)} %copy-done.5) | copy-start | bytes 884740
  91.9 9.6 %copy-start.4 = (bf16[96,1536]{1,0:T(8,128)(2,1)S(1)}, bf16[96,1536]{1,0:T(8,128)(2,1)}, u32[]{:S(2)}) copy-start(bf16[96,1536]{1,0:T(8,128)(2,1)} %copy-done.3) | copy-start | bytes 884740
  91.9 15.6 %copy-start.11 = (s32[1,16]{1,0:T(1,128)S(1)}, s32[1,16]{1,0:T(1,128)}, u32[]{:S(2)}) copy-start(s32[1,16]{1,0:T(1,128)} %param.16) | copy-start | bytes 196
  93.0 15.7 %all-to-all-start.2 = ((bf16[16,2,11136]{2,1,0:T(2,128)(2,1)}), bf16[16,2,11136]{2,1,0:T(2,128)(2,1)}, u32[]{:S(2)}, u32[]{:S(2)}) async-start(bf16[16,2,11136]{2,1,0:T(2,128)(2,1)} %reshape.187), calls=%async_computation.2 | async-start | bytes 1425408 | tf_op jit(solution)/shard_map/all_to_all | solution.py:164
  102.2 40.3 %collective-permute-start.14 = (bf16[8,96,1536]{2,1,0:T(8,128)(2,1)}, bf16[8,96,1536]{2,1,0:T(8,128)(2,1)}, u32[]{:S(2)}, u32[]{:S(2)}) collective-permute-start(bf16[8,96,1536]{2,1,0:T(8,128)(2,1)} %bitcast_dynamic-update-slice_fusion), channel_id=1, source_target_pairs={{0,128},{128,0},{1,129},{129,1},{2,130},{130,2},{3,131},{131,3},{4... | collective-permute-start | bytes 7077896 | tf_op jit(solution)/shard_map/ppermute | solution.py:108
  124.0 14.5 %all-to-all-start.3 = ((bf16[16,32,192]{2,1,0:T(8,128)(2,1)}), bf16[16,32,192]{2,1,0:T(8,128)(2,1)}, u32[]{:S(2)}, u32[]{:S(2)}) async-start(bf16[16,32,192]{2,1,0:T(8,128)(2,1)} %reshape.178), calls=%async_computation.3 | async-start | bytes 524288 | tf_op jit(solution)/shard_map/all_to_all | solution.py:181
  138.4 13.5 %all-to-all-start.4 = ((bf16[8,2,32,192]{3,2,1,0:T(8,128)(2,1)}), bf16[8,2,32,192]{3,2,1,0:T(8,128)(2,1)S(1)}, u32[]{:S(2)}, u32[]{:S(2)}) async-start(bf16[8,2,32,192]{3,2,1,0:T(8,128)(2,1)} %bitcast.24), calls=%async_computation.4 | async-start | bytes 524288 | tf_op jit(solution)/shard_map/all_to_all | solution.py:182
  156.2 38.9 %copy-start.10 = (bf16[384,1536]{1,0:T(8,128)(2,1)S(1)}, bf16[384,1536]{1,0:T(8,128)(2,1)}, u32[]{:S(2)}) copy-start(bf16[384,1536]{1,0:T(8,128)(2,1)} %param.26) | copy-start | bytes 3538948
  202.6 4.6 %copy-start.9 = (f32[2,32,32]{2,1,0:T(8,128)S(1)}, f32[2,32,32]{2,1,0:T(8,128)}, u32[]{:S(2)}) copy-start(f32[2,32,32]{2,1,0:T(8,128)} %param.19) | copy-start | bytes 24580
  202.6 40.3 %all-to-all-start.6 = ((bf16[16,2,32,1536]{3,2,1,0:T(8,128)(2,1)}), bf16[16,2,32,1536]{3,2,1,0:T(8,128)(2,1)}, u32[]{:S(2)}, u32[]{:S(2)}) async-start(bf16[16,2,32,1536]{3,2,1,0:T(8,128)(2,1)} %convolution_convert_fusion), calls=%async_computation.6 | async-start | bytes 6291456 | tf_op jit(solution)/shard_map/all_to_all | solution.py:197
  207.2 46.8 %collective-permute-start.16 = (f32[2,32,32]{2,1,0:T(8,128)S(1)}, f32[2,32,32]{2,1,0:T(8,128)S(1)}, u32[]{:S(2)}, u32[]{:S(2)}) collective-permute-start(f32[2,32,32]{2,1,0:T(8,128)S(1)} %copy-done.9), channel_id=1, source_target_pairs={{0,128},{128,0},{1,129},{129,1},{2,130},{130,2},{3,131},{131,3},{4... | collective-permute-start | bytes 24584 | tf_op jit(solution)/shard_map/ppermute | solution.py:117
  212.8 32.8 %copy-start.7 = (bf16[1536,64]{0,1:T(8,128)(2,1)S(1)}, bf16[1536,64]{0,1:T(8,128)(2,1)}, u32[]{:S(2)}) copy-start(bf16[1536,64]{0,1:T(8,128)(2,1)} %param.27) | copy-start | bytes 589828
  245.9 8.9 %collective-permute-start.15 = (f32[2,32,64]{2,1,0:T(8,128)S(1)}, f32[2,32,64]{2,1,0:T(8,128)S(1)}, u32[]{:S(2)}, u32[]{:S(2)}) collective-permute-start(f32[2,32,64]{2,1,0:T(8,128)S(1)} %fusion.66), channel_id=1, source_target_pairs={{0,128},{128,0},{1,129},{129,1},{2,130},{130,2},{3,131},{131,3},{4... | collective-permute-start | bytes 49160 | tf_op jit(solution)/shard_map/ppermute | solution.py:204
  255.0 2.5 collective-permute-start.17
  257.6 4.0 %collective-permute-start.18 = (f32[2,2]{1,0:T(2,128)S(1)}, f32[2,2]{1,0:T(2,128)S(1)}, u32[]{:S(2)}, u32[]{:S(2)}) collective-permute-start(f32[2,2]{1,0:T(2,128)S(1)} %pad_maximum_fusion.4), channel_id=1, source_target_pairs={{0,2},{1,3},{2,0},{3,1},{4,6},{5,7},{6,4},{7,5},{8,10},{9,11},{10,... | collective-permute-start | bytes 56 | tf_op jit(solution)/shard_map/ppermute | solution.py:215
  261.6 2.5 collective-permute-start.19
  264.1 4.0 %collective-permute-start.20 = (f32[2,2]{1,0:T(2,128)S(1)}, f32[2,2]{1,0:T(2,128)S(1)}, u32[]{:S(2)}, u32[]{:S(2)}) collective-permute-start(f32[2,2]{1,0:T(2,128)S(1)} %pad_maximum_fusion.6), channel_id=1, source_target_pairs={{0,8},{1,9},{2,10},{3,11},{4,12},{5,13},{6,14},{7,15},{8,0},{9,1},... | collective-permute-start | bytes 56 | tf_op jit(solution)/shard_map/ppermute | solution.py:215
where the time goes:
time: 272 us; the launch traced here: 269 us
  waiting for transfers between devices  96.8 us (36%)
  starting transfers between devices  64.4 us (24%)
  blocking collectives  38.9 us (14%)
  local copies, waits for them, and re-layouts  23.8 us (9%)
  matrix products  23.7 us (9%)
  other arithmetic  19.9 us (7%)
    all_to_all x1, blocking collectives, gather_by_a2a(): return lax.all_to_all(copies, axis, 0, 0, tiled=True)  38.9 us
    all_to_all x1, waiting for transfers between devices, on_device(): block_terms = lax.all_to_all(mlp_terms, 'seq', 0, 0, tiled=True)  30.1 us
    ppermute x8, waiting for transfers between devices, ring_gather(): from_below = lax.ppermute(from_below, axis, up)  24.3 us
    unnamed x47, local copies, waits for them, and re-layouts  15.3 us
    ppermute x6, starting transfers between devices, ring_gather(): from_above = lax.ppermute(from_above, axis, down)  12.7 us
    ppermute x4, waiting for transfers between devices, on_device(): lax.ppermute(jnp.stack([squares, largest]), 'seq', xor_pairs('seq', dista...  10.7 us
    ppermute x6, waiting for transfers between devices, ring_gather(): from_above = lax.ppermute(from_above, axis, down)  9.49 us
    ppermute x1, starting transfers between devices, on_device(): other_velocity = lax.ppermute(own_velocity, 'cfg', xor_pairs('cfg', 1))  8.06 us
  transfers between devices with their start and end apart: 27, of which 16 were waited for; matrix products, arithmetic and copies ran while one was open for 19% of the time, Pallas kernels for 0%

commit v1 on v0

--- a/solution.py
+++ b/solution.py
@@ -52,13 +52,15 @@
     return lax.all_to_all(copies, axis, 0, 0, tiled=True)
 
 
-def ring_gather(value, axis):
+def ring_gather(value, axis, after=None):
     count = lax.axis_size(axis)
     up = [(source, (source + 1) % count) for source in range(count)]
     down = [(source, (source - 1) % count) for source in range(count)]
     ahead = {0: value}
     from_below, from_above = value, value
     for step in range(1, count // 2 + 1):
+        if step == 2 and after is not None:
+            from_below, from_above, _ = lax.optimization_barrier((from_below, from_above, after))
         from_below = lax.ppermute(from_below, axis, up)
         ahead[count - step] = from_below
         if step < count - step:
@@ -102,17 +104,6 @@
     seq_count = lax.axis_size("seq")
     half_index = lax.axis_index("cfg")
     cond_first = half_index == 0
-    split_rows = out_weight.shape[0] // 2
-    own_part = lax.dynamic_slice_in_dim(out_weight, half_index * split_rows, split_rows, 0)
-    gathered_part = ring_gather(own_part, "req")
-    partner_part = lax.ppermute(gathered_part, "cfg", xor_pairs("cfg", 1))
-    every_weight = jnp.concatenate(
-        [
-            jnp.where(cond_first, gathered_part, partner_part),
-            jnp.where(cond_first, partner_part, gathered_part),
-        ],
-        axis=1,
-    )
     half_values = latent.shape[2]
     partner_latent = lax.ppermute(latent, "cfg", xor_pairs("cfg", 1))
     full_latent = jnp.concatenate(
@@ -145,6 +136,17 @@
     text_block = txt_in.shape[1]
     both = ring_gather(jnp.concatenate([img_in, txt_in], axis=1), "req")
     both = both.reshape(req_count * group_size, row_count + text_block, D)
+    split_rows = out_weight.shape[0] // 2
+    own_part = lax.dynamic_slice_in_dim(out_weight, half_index * split_rows, split_rows, 0)
+    gathered_part = ring_gather(own_part, "req", after=both)
+    partner_part = lax.ppermute(gathered_part, "cfg", xor_pairs("cfg", 1))
+    every_weight = jnp.concatenate(
+        [
+            jnp.where(cond_first, gathered_part, partner_part),
+            jnp.where(cond_first, partner_part, gathered_part),
+        ],
+        axis=1,
+    )
     head_width = img_qkv.shape[2]
     local_heads = head_width // HD
     qkv_columns = img_qkv.reshape(D, 3 * head_width)

time: 272 us -> 289 us (1.062)
  waiting for transfers between devices: 96.8 us -> 109 us
    ppermute x8, waiting for transfers between devices: 24.3 us -> 31.2 us  [ring_gather(): from_below = lax.ppermute(from_below, axis, up)]
    ppermute x1, starting transfers between devices: 5.26 us -> 11.1 us  [on_device(): partner_part = lax.ppermute(gathered_part, 'cfg', xor_pairs('cfg', 1))]
    all_to_all x1, waiting for transfers between devices: 30.1 us -> 34.5 us  [on_device(): block_terms = lax.all_to_all(mlp_terms, 'seq', 0, 0, tiled=True)]
    unnamed x47 -> x39, local copies, waits for them, and re-layouts: 15.3 us -> 16.3 us
  transfers between devices with their start and end apart: 27 -> 27, of which waited for: 16 -> 17; matrix products, arithmetic and copies ran while one was open for 19% -> 19% of each run, Pallas kernels for 0% -> 0%
where the time goes in v1:
time: 289 us; the launch traced here: 286 us
  waiting for transfers between devices  109 us (38%)
  starting transfers between devices  65.8 us (23%)
  blocking collectives  40.8 us (14%)
  local copies, waits for them, and re-layouts  25.7 us (9%)
  matrix products  23.8 us (8%)
  other arithmetic  19.9 us (7%)
    all_to_all x1, blocking collectives, gather_by_a2a(): return lax.all_to_all(copies, axis, 0, 0, tiled=True)  40.8 us
    all_to_all x1, waiting for transfers between devices, on_device(): block_terms = lax.all_to_all(mlp_terms, 'seq', 0, 0, tiled=True)  34.5 us
    ppermute x8, waiting for transfers between devices, ring_gather(): from_below = lax.ppermute(from_below, axis, up)  31.2 us
    unnamed x39, local copies, waits for them, and re-layouts  16.3 us
    ppermute x6, starting transfers between devices, ring_gather(): from_above = lax.ppermute(from_above, axis, down)  11.2 us
    ppermute x1, starting transfers between devices, on_device(): partner_part = lax.ppermute(gathered_part, 'cfg', xor_pairs('cfg', 1))  11.1 us
    ppermute x4, waiting for transfers between devices, on_device(): lax.ppermute(jnp.stack([squares, largest]), 'seq', xor_pairs('seq', dista...  10.5 us
    ppermute x6, waiting for transfers between devices, ring_gather(): from_above = lax.ppermute(from_above, axis, down)  8.69 us
  transfers between devices with their start and end apart: 27, of which 17 were waited for; matrix products, arithmetic and copies ran while one was open for 19% of the time, Pallas kernels for 0%

profile of v1, /device:TPU:1, one launch (start us, length us, event | category | flops | bytes accessed | tf_op | source)
XLA Modules:
  0.0 285.8 jit_solution(16643303793295520145)
XLA Ops:
  0.7 2.0 bitcast_dynamic-update-slice_fusion.7
  2.7 6.4 %collective-permute-start.7 = (bf16[96,1536]{1,0:T(8,128)(2,1)}, bf16[96,1536]{1,0:T(8,128)(2,1)}, u32[]{:S(2)}, u32[]{:S(2)}) collective-permute-start(bf16[96,1536]{1,0:T(8,128)(2,1)} %get-tuple-element.17), channel_id=1, source_target_pairs={{0,112},{16,0},{32,16},{48,32},{64,48},{80,64},{96,80},{112,96},{1... | collective-permute-start | bytes 884744 | tf_op jit(solution)/shard_map/ppermute | solution.py:67
  10.0 1.8 convolution_add_fusion
  11.8 4.1 %all-to-all-start = ((f32[8,2,120]{2,1,0:T(2,128)}), f32[8,2,120]{2,1,0:T(2,128)S(1)}, u32[]{:S(2)}, u32[]{:S(2)}) async-start(f32[8,2,120]{2,1,0:T(2,128)} %bitcast.2), calls=%async_computation | async-start | bytes 16384 | tf_op jit(solution)/shard_map/all_to_all | solution.py:120
  20.0 2.5 all-to-all-done
  23.2 6.8 %all-to-all-start.1 = ((f32[16,8,2,120]{3,1,2,0:T(8,128)}), f32[16,8,2,120]{3,1,2,0:T(8,128)S(1)}, u32[]{:S(2)}, u32[]{:S(2)}) async-start(f32[16,8,2,120]{3,1,2,0:T(8,128)} %broadcast_in_dim.12), calls=%async_computation.1 | async-start | bytes 262144 | tf_op jit(solution)/shard_map/all_to_all | solution.py:52
  29.9 6.8 %all-to-all-done.1 = f32[16,8,2,120]{3,1,2,0:T(8,128)S(1)} async-done(((f32[16,8,2,120]{3,1,2,0:T(8,128)}), f32[16,8,2,120]{3,1,2,0:T(8,128)S(1)}, u32[]{:S(2)}, u32[]{:S(2)}) %all-to-all-start.1) | async-done | bytes 122912 | tf_op jit(solution)/shard_map/all_to_all | solution.py:52
  37.8 1.2 collective-permute-start.3
  39.0 1.7 bitcast_dynamic-update-slice_fusion.6
  40.7 2.4 collective-permute-done
  43.1 1.5 collective-permute-start.1
  44.6 6.3 %collective-permute-done.1 = bf16[2,42,1536]{2,1,0:T(8,128)(2,1)S(1)} collective-permute-done((bf16[2,42,1536]{2,1,0:T(8,128)(2,1)S(1)}, bf16[2,42,1536]{2,1,0:T(8,128)(2,1)S(1)}, u32[]{:S(2)}, u32[]{:S(2)}) %collective-permute-start.1) | collective-permute-done | bytes 258080 | tf_op jit(solution)/shard_map/ppermute | solution.py:67
  50.9 1.4 collective-permute-start.2
  52.6 9.1 %collective-permute-done.5 = bf16[2,42,1536]{2,1,0:T(8,128)(2,1)S(1)} collective-permute-done((bf16[2,42,1536]{2,1,0:T(8,128)(2,1)S(1)}, bf16[2,42,1536]{2,1,0:T(8,128)(2,1)S(1)}, u32[]{:S(2)}, u32[]{:S(2)}) %collective-permute-start.5) | collective-permute-done | bytes 258080 | tf_op jit(solution)/shard_map/ppermute | solution.py:64
  61.7 9.9 %collective-permute-done.6 = bf16[2,42,1536]{2,1,0:T(8,128)(2,1)S(1)} collective-permute-done((bf16[2,42,1536]{2,1,0:T(8,128)(2,1)S(1)}, bf16[2,42,1536]{2,1,0:T(8,128)(2,1)S(1)}, u32[]{:S(2)}, u32[]{:S(2)}) %collective-permute-start.6) | collective-permute-done | bytes 258080 | tf_op jit(solution)/shard_map/ppermute | solution.py:64
  71.7 1.4 copy-done.4
  73.1 1.4 fusion.30
  75.3 2.1 convolution_convert_fusion.1
  77.6 1.5 collective-permute-start.11
  79.0 3.2 %fusion.46 = bf16[16,1,22272]{2,0,1:T(8,128)(2,1)S(1)} fusion(s32[]{:T(128)S(6)} %select_n.79, bf16[16,18432]{1,0:T(8,128)(2,1)S(1)} %reshape.170, bf16[16,3840]{1,0:T(8,128)(2,1)S(1)} %bitcast.204), kind=kLoop, calls=%fused_computation.50 | loop fusion | flops 2850816 | bytes 1425412 | tf_op jit(solution)/shard_map/all_to_all | solution.py:166
  82.8 1.2 reduce.2
  85.0 4.4 %all-to-all-start.2 = ((bf16[16,2,11136]{2,1,0:T(2,128)(2,1)}), bf16[16,2,11136]{2,1,0:T(2,128)(2,1)}, u32[]{:S(2)}, u32[]{:S(2)}) async-start(bf16[16,2,11136]{2,1,0:T(2,128)(2,1)} %reshape.187), calls=%async_computation.2 | async-start | bytes 1425408 | tf_op jit(solution)/shard_map/all_to_all | solution.py:166
  89.4 1.6 collective-permute-start.10
  90.9 1.7 bitcast_dynamic-update-slice_fusion.5
  92.7 5.3 %collective-permute-done.12 = bf16[96,1536]{1,0:T(8,128)(2,1)S(1)} collective-permute-done((bf16[96,1536]{1,0:T(8,128)(2,1)}, bf16[96,1536]{1,0:T(8,128)(2,1)S(1)}, u32[]{:S(2)}, u32[]{:S(2)}) %collective-permute-start.12) | collective-permute-done | bytes 294944 | tf_op jit(solution)/shard_map/ppermute | solution.py:64
  98.7 6.7 %collective-permute-done.13 = bf16[96,1536]{1,0:T(8,128)(2,1)S(1)} collective-permute-done((bf16[96,1536]{1,0:T(8,128)(2,1)S(1)}, bf16[96,1536]{1,0:T(8,128)(2,1)S(1)}, u32[]{:S(2)}, u32[]{:S(2)}) %collective-permute-start.13) | collective-permute-done | bytes 294944 | tf_op jit(solution)/shard_map/ppermute | solution.py:64
  106.8 1.7 bitcast_dynamic-update-slice_fusion.1
  108.6 1.7 bitcast_dynamic-update-slice_fusion
  110.3 11.1 %collective-permute-start.14 = (bf16[8,96,1536]{2,1,0:T(8,128)(2,1)}, bf16[8,96,1536]{2,1,0:T(8,128)(2,1)}, u32[]{:S(2)}, u32[]{:S(2)}) collective-permute-start(bf16[8,96,1536]{2,1,0:T(8,128)(2,1)} %bitcast_dynamic-update-slice_fusion), channel_id=1, source_target_pairs={{0,128},{128,0},{1,129},{129,1},{2,130},{130,2},{3,131},{131,3},{4... | collective-permute-start | bytes 7077896 | tf_op jit(solution)/shard_map/ppermute | solution.py:142
  122.6 4.2 %reshape.188 = bf16[16,1,22272]{2,1,0:T(2,128)(2,1)S(1)} reshape(bf16[16,2,11136]{2,1,0:T(2,128)(2,1)} %all-to-all-done.2) | data formatting | bytes 1425408
  129.4 4.6 %fusion.89 = (f32[3,512]{1,0:T(4,128)S(1)}, f32[3,512,672]{1,2,0:T(8,128)}) fusion(pred[672]{0:T(1024)(128)(4,1)S(1)} %iota_compare_fusion, bf16[512,3,64]{0,2,1:T(8,128)(2,1)} %bitcast.207, bf16[672,3,64]{0,2,1:T(8,128)(2,1)S(1)} %bitcast.205), kind=kOutput, calls=%fused_computation.181 | convolution fusion | flops 136250016 | bytes 4590240 | tf_op jit(solution)/shard_map/sub | solution.py:80
  134.0 2.7 fusion.36
  138.0 6.6 %all-to-all-start.3 = ((bf16[16,32,192]{2,1,0:T(8,128)(2,1)}), bf16[16,32,192]{2,1,0:T(8,128)(2,1)}, u32[]{:S(2)}, u32[]{:S(2)}) async-start(bf16[16,32,192]{2,1,0:T(8,128)(2,1)} %reshape.178), calls=%async_computation.3 | async-start | bytes 524288 | tf_op jit(solution)/shard_map/all_to_all | solution.py:183
  144.7 8.5 %all-to-all-done.3 = bf16[16,32,192]{2,1,0:T(8,128)(2,1)} async-done(((bf16[16,32,192]{2,1,0:T(8,128)(2,1)}), bf16[16,32,192]{2,1,0:T(8,128)(2,1)}, u32[]{:S(2)}, u32[]{:S(2)}) %all-to-all-start.3) | async-done | bytes 196640 | tf_op jit(solution)/shard_map/all_to_all | solution.py:183
  153.2 3.4 %all-to-all-start.4 = ((bf16[8,2,32,192]{3,2,1,0:T(8,128)(2,1)}), bf16[8,2,32,192]{3,2,1,0:T(8,128)(2,1)S(1)}, u32[]{:S(2)}, u32[]{:S(2)}) async-start(bf16[8,2,32,192]{3,2,1,0:T(8,128)(2,1)} %bitcast.24), calls=%async_computation.4 | async-start | bytes 524288 | tf_op jit(solution)/shard_map/all_to_all | solution.py:184
  156.6 4.9 %broadcast_select_fusion.1 = (bf16[8,96,1536]{2,1,0:T(8,128)(2,1)}, bf16[8,96,1536]{2,1,0:T(8,128)(2,1)}) fusion(bf16[8,96,1536]{2,1,0:T(8,128)(2,1)} %bitcast_dynamic-update-slice_fusion, bf16[8,96,1536]{2,1,0:T(8,128)(2,1)} %collective-permute-done.14, pred[]{:T(512)S(6)} %eq.8), kind=kLoop, calls=%fused_computation.14 | loop fusion | flops 2359296 | bytes 9437185 | tf_op jit(solution)/shard_map/jit(_where)/select_n | solution.py:145
  161.5 5.2 %all-to-all-done.4 = bf16[8,2,32,192]{3,2,1,0:T(8,128)(2,1)S(1)} async-done(((bf16[8,2,32,192]{3,2,1,0:T(8,128)(2,1)}), bf16[8,2,32,192]{3,2,1,0:T(8,128)(2,1)S(1)}, u32[]{:S(2)}, u32[]{:S(2)}) %all-to-all-start.4) | async-done | bytes 196640 | tf_op jit(solution)/shard_map/all_to_all | solution.py:184
  166.7 3.4 %fusion.90 = (f32[2,32]{1,0:T(2,128)S(1)}, f32[2,32,1536]{2,1,0:T(8,128)S(1)}) fusion(bf16[8,96,1536]{2,1,0:T(8,128)(2,1)} %get-tuple-element.19, bf16[8,96,1536]{2,1,0:T(8,128)(2,1)} %get-tuple-element.18, s32[]{:T(128)S(6)} %select_n.83, bf16[8,2,32,192]{3,2,1,0:T(8,128)(2,1)S(1)} %all-to-all-done.4, f32[2,1536]{1,0:T(2,128)S(1)} %bitcast.212, ...), kind=kOutput, calls=%fused_computation.182 | convolution fusion | flops 311918528 | bytes 5517572 | tf_op jit(solution)/shard_map/grnk,gkd->rnd/dot_general | solution.py:188
  170.9 40.8 %all_to_all.42 = bf16[16,2,32,1536]{3,2,1,0:T(8,128)(2,1)} all-to-all(bf16[16,2,32,1536]{3,2,1,0:T(8,128)(2,1)S(1)} %broadcast_in_dim.15), channel_id=1, replica_groups=mesh['cfg'=2,'req'=8,'seq'=16] {'seq'}, dimensions={0} | all-to-all | bytes 6291456 | tf_op jit(solution)/shard_map/all_to_all | solution.py:52
  211.7 7.5 %convolution_convert_fusion = bf16[16,2,32,1536]{3,2,1,0:T(8,128)(2,1)} fusion(bf16[384,1536]{1,0:T(8,128)(2,1)S(1)} %copy-done.6, bf16[16,2,32,1536]{3,2,1,0:T(8,128)(2,1)} %all_to_all.42, bf16[1536,384]{1,0:T(8,128)(2,1)} %param.25), kind=kOutput, calls=%fused_computation.10 | convolution fusion | flops 2421030912 | bytes 8650752 | tf_op jit(solution)/shard_map/srnf,fd->srnd/dot_general | solution.py:196
  219.2 4.6 %all-to-all-start.6 = ((bf16[16,2,32,1536]{3,2,1,0:T(8,128)(2,1)}), bf16[16,2,32,1536]{3,2,1,0:T(8,128)(2,1)}, u32[]{:S(2)}, u32[]{:S(2)}) async-start(bf16[16,2,32,1536]{3,2,1,0:T(8,128)(2,1)} %convolution_convert_fusion), calls=%async_computation.6 | async-start | bytes 6291456 | tf_op jit(solution)/shard_map/all_to_all | solution.py:199
  223.8 3.6 %collective-permute-start.16 = (f32[2,32,32]{2,1,0:T(8,128)S(1)}, f32[2,32,32]{2,1,0:T(8,128)S(1)}, u32[]{:S(2)}, u32[]{:S(2)}) collective-permute-start(f32[2,32,32]{2,1,0:T(8,128)S(1)} %copy-done.5), channel_id=1, source_target_pairs={{0,128},{128,0},{1,129},{129,1},{2,130},{130,2},{3,131},{131,3},{4... | collective-permute-start | bytes 24584 | tf_op jit(solution)/shard_map/ppermute | solution.py:108
  227.5 34.5 %all-to-all-done.6 = bf16[16,2,32,1536]{3,2,1,0:T(8,128)(2,1)} async-done(((bf16[16,2,32,1536]{3,2,1,0:T(8,128)(2,1)}), bf16[16,2,32,1536]{3,2,1,0:T(8,128)(2,1)}, u32[]{:S(2)}, u32[]{:S(2)}) %all-to-all-start.6) | async-done | bytes 3145760 | tf_op jit(solution)/shard_map/all_to_all | solution.py:199
  262.0 2.4 convert_reduce_fusion
  265.0 6.1 %collective-permute-start.15 = (f32[2,32,64]{2,1,0:T(8,128)S(1)}, f32[2,32,64]{2,1,0:T(8,128)S(1)}, u32[]{:S(2)}, u32[]{:S(2)}) collective-permute-start(f32[2,32,64]{2,1,0:T(8,128)S(1)} %fusion.66), channel_id=1, source_target_pairs={{0,128},{128,0},{1,129},{129,1},{2,130},{130,2},{3,131},{131,3},{4... | collective-permute-start | bytes 49160 | tf_op jit(solution)/shard_map/ppermute | solution.py:206
  274.8 3.9 %collective-permute-done.18 = f32[2,2]{1,0:T(2,128)S(1)} collective-permute-done((f32[2,2]{1,0:T(2,128)S(1)}, f32[2,2]{1,0:T(2,128)S(1)}, u32[]{:S(2)}, u32[]{:S(2)}) %collective-permute-start.18) | collective-permute-done | bytes 48 | tf_op jit(solution)/shard_map/ppermute | solution.py:217
  278.9 2.4 collective-permute-done.19
  282.2 3.1 %collective-permute-done.20 = f32[2,2]{1,0:T(2,128)S(1)} collective-permute-done((f32[2,2]{1,0:T(2,128)S(1)}, f32[2,2]{1,0:T(2,128)S(1)}, u32[]{:S(2)}, u32[]{:S(2)}) %collective-permute-start.20) | collective-permute-done | bytes 48 | tf_op jit(solution)/shard_map/ppermute | solution.py:217
  (120 shorter events, 23.6 us)
Async XLA Ops:
  0.6 71.1 %copy-start = (bf16[1536,3,192]{0,2,1:T(8,128)(2,1)S(1)}, bf16[1536,3,192]{0,2,1:T(8,128)(2,1)}, u32[]{:S(2)}) copy-start(bf16[1536,3,192]{0,2,1:T(8,128)(2,1)} %param.22) | copy-start | bytes 5308420
  0.6 36.5 %copy-start.1 = (bf16[1,2,32,1536]{3,2,1,0:T(8,128)(2,1)S(1)}, bf16[1,2,32,1536]{3,2,1,0:T(8,128)(2,1)}, u32[]{:S(2)}) copy-start(bf16[1,2,32,1536]{3,2,1,0:T(8,128)(2,1)} %param.14) | copy-start | bytes 589828
  0.7 36.6 %copy-start.2 = (bf16[1,2,10,1536]{3,1,2,0:T(2,128)(2,1)S(1)}, bf16[1,2,10,1536]{3,1,2,0:T(2,128)(2,1)}, u32[]{:S(2)}) copy-start(bf16[1,2,10,1536]{3,1,2,0:T(2,128)(2,1)} %param.15) | copy-start | bytes 184324
  2.7 36.3 %collective-permute-start.7 = (bf16[96,1536]{1,0:T(8,128)(2,1)}, bf16[96,1536]{1,0:T(8,128)(2,1)}, u32[]{:S(2)}, u32[]{:S(2)}) collective-permute-start(bf16[96,1536]{1,0:T(8,128)(2,1)} %get-tuple-element.17), channel_id=1, source_target_pairs={{0,112},{16,0},{32,16},{48,32},{64,48},{80,64},{96,80},{112,96},{1... | collective-permute-start | bytes 884744 | tf_op jit(solution)/shard_map/ppermute | solution.py:67
  9.1 68.4 %collective-permute-start.8 = (bf16[96,1536]{1,0:T(8,128)(2,1)}, bf16[96,1536]{1,0:T(8,128)(2,1)}, u32[]{:S(2)}, u32[]{:S(2)}) collective-permute-start(bf16[96,1536]{1,0:T(8,128)(2,1)} %get-tuple-element.17), channel_id=1, source_target_pairs={{0,16},{16,32},{32,48},{48,64},{64,80},{80,96},{96,112},{112,0},{1... | collective-permute-start | bytes 884744 | tf_op jit(solution)/shard_map/ppermute | solution.py:64
  11.8 10.7 %all-to-all-start = ((f32[8,2,120]{2,1,0:T(2,128)}), f32[8,2,120]{2,1,0:T(2,128)S(1)}, u32[]{:S(2)}, u32[]{:S(2)}) async-start(f32[8,2,120]{2,1,0:T(2,128)} %bitcast.2), calls=%async_computation | async-start | bytes 16384 | tf_op jit(solution)/shard_map/all_to_all | solution.py:120
  23.2 13.6 %all-to-all-start.1 = ((f32[16,8,2,120]{3,1,2,0:T(8,128)}), f32[16,8,2,120]{3,1,2,0:T(8,128)S(1)}, u32[]{:S(2)}, u32[]{:S(2)}) async-start(f32[16,8,2,120]{3,1,2,0:T(8,128)} %broadcast_in_dim.12), calls=%async_computation.1 | async-start | bytes 262144 | tf_op jit(solution)/shard_map/all_to_all | solution.py:52
  37.4 5.7 %collective-permute-start = (bf16[2,42,1536]{2,1,0:T(8,128)(2,1)S(1)}, bf16[2,42,1536]{2,1,0:T(8,128)(2,1)S(1)}, u32[]{:S(2)}, u32[]{:S(2)}) collective-permute-start(bf16[2,42,1536]{2,1,0:T(8,128)(2,1)S(1)} %pad_maximum_fusion.2), channel_id=1, source_target_pairs={{0,112},{16,0},{32,16},{48,32},{64,48},{80,64},{96,80},{112,96},{1... | collective-permute-start | bytes 774152 | tf_op jit(solution)/shard_map/ppermute | solution.py:67
  37.8 6.8 %collective-permute-start.3 = (bf16[2,42,1536]{2,1,0:T(8,128)(2,1)S(1)}, bf16[2,42,1536]{2,1,0:T(8,128)(2,1)S(1)}, u32[]{:S(2)}, u32[]{:S(2)}) collective-permute-start(bf16[2,42,1536]{2,1,0:T(8,128)(2,1)S(1)} %pad_maximum_fusion.2), channel_id=1, source_target_pairs={{0,16},{16,32},{32,48},{48,64},{64,80},{80,96},{96,112},{112,0},{1... | collective-permute-start | bytes 774152 | tf_op jit(solution)/shard_map/ppermute | solution.py:64
  43.1 7.8 %collective-permute-start.1 = (bf16[2,42,1536]{2,1,0:T(8,128)(2,1)S(1)}, bf16[2,42,1536]{2,1,0:T(8,128)(2,1)S(1)}, u32[]{:S(2)}, u32[]{:S(2)}) collective-permute-start(bf16[2,42,1536]{2,1,0:T(8,128)(2,1)S(1)} %collective-permute-done), channel_id=1, source_target_pairs={{0,112},{16,0},{32,16},{48,32},{64,48},{80,64},{96,80},{112,96},{1... | collective-permute-start | bytes 774152 | tf_op jit(solution)/shard_map/ppermute | solution.py:67
  44.6 8.0 %collective-permute-start.4 = (bf16[2,42,1536]{2,1,0:T(8,128)(2,1)S(1)}, bf16[2,42,1536]{2,1,0:T(8,128)(2,1)S(1)}, u32[]{:S(2)}, u32[]{:S(2)}) collective-permute-start(bf16[2,42,1536]{2,1,0:T(8,128)(2,1)S(1)} %collective-permute-done.3), channel_id=1, source_target_pairs={{0,16},{16,32},{32,48},{48,64},{64,80},{80,96},{96,112},{112,0},{1... | collective-permute-start | bytes 774152 | tf_op jit(solution)/shard_map/ppermute | solution.py:64
  50.9 10.8 %collective-permute-start.2 = (bf16[2,42,1536]{2,1,0:T(8,128)(2,1)S(1)}, bf16[2,42,1536]{2,1,0:T(8,128)(2,1)S(1)}, u32[]{:S(2)}, u32[]{:S(2)}) collective-permute-start(bf16[2,42,1536]{2,1,0:T(8,128)(2,1)S(1)} %collective-permute-done.1), channel_id=1, source_target_pairs={{0,112},{16,0},{32,16},{48,32},{64,48},{80,64},{96,80},{112,96},{1... | collective-permute-start | bytes 774152 | tf_op jit(solution)/shard_map/ppermute | solution.py:67
  52.5 9.1 %collective-permute-start.5 = (bf16[2,42,1536]{2,1,0:T(8,128)(2,1)S(1)}, bf16[2,42,1536]{2,1,0:T(8,128)(2,1)S(1)}, u32[]{:S(2)}, u32[]{:S(2)}) collective-permute-start(bf16[2,42,1536]{2,1,0:T(8,128)(2,1)S(1)} %collective-permute-done.4), channel_id=1, source_target_pairs={{0,16},{16,32},{32,48},{48,64},{64,80},{80,96},{96,112},{112,0},{1... | collective-permute-start | bytes 774152 | tf_op jit(solution)/shard_map/ppermute | solution.py:64
  61.7 9.9 %collective-permute-start.6 = (bf16[2,42,1536]{2,1,0:T(8,128)(2,1)S(1)}, bf16[2,42,1536]{2,1,0:T(8,128)(2,1)S(1)}, u32[]{:S(2)}, u32[]{:S(2)}) collective-permute-start(bf16[2,42,1536]{2,1,0:T(8,128)(2,1)S(1)} %collective-permute-done.5), channel_id=1, source_target_pairs={{0,16},{16,32},{32,48},{48,64},{64,80},{80,96},{96,112},{112,0},{1... | collective-permute-start | bytes 774152 | tf_op jit(solution)/shard_map/ppermute | solution.py:64
  71.7 1.5 copy-start.4
  77.5 11.9 %collective-permute-start.9 = (bf16[96,1536]{1,0:T(8,128)(2,1)}, bf16[96,1536]{1,0:T(8,128)(2,1)}, u32[]{:S(2)}, u32[]{:S(2)}) collective-permute-start(bf16[96,1536]{1,0:T(8,128)(2,1)} %collective-permute-done.7), channel_id=1, source_target_pairs={{0,112},{16,0},{32,16},{48,32},{64,48},{80,64},{96,80},{112,96},{1... | collective-permute-start | bytes 884744 | tf_op jit(solution)/shard_map/ppermute | solution.py:67
  77.6 13.3 %collective-permute-start.11 = (bf16[96,1536]{1,0:T(8,128)(2,1)}, bf16[96,1536]{1,0:T(8,128)(2,1)}, u32[]{:S(2)}, u32[]{:S(2)}) collective-permute-start(bf16[96,1536]{1,0:T(8,128)(2,1)} %collective-permute-done.8), channel_id=1, source_target_pairs={{0,16},{16,32},{32,48},{48,64},{64,80},{80,96},{96,112},{112,0},{1... | collective-permute-start | bytes 884744 | tf_op jit(solution)/shard_map/ppermute | solution.py:64
  85.0 36.4 %copy-start.7 = (s32[1,16]{1,0:T(1,128)S(1)}, s32[1,16]{1,0:T(1,128)}, u32[]{:S(2)}) copy-start(s32[1,16]{1,0:T(1,128)} %param.16) | copy-start | bytes 196
  85.0 37.7 %all-to-all-start.2 = ((bf16[16,2,11136]{2,1,0:T(2,128)(2,1)}), bf16[16,2,11136]{2,1,0:T(2,128)(2,1)}, u32[]{:S(2)}, u32[]{:S(2)}) async-start(bf16[16,2,11136]{2,1,0:T(2,128)(2,1)} %reshape.187), calls=%async_computation.2 | async-start | bytes 1425408 | tf_op jit(solution)/shard_map/all_to_all | solution.py:166
  89.4 8.6 %collective-permute-start.10 = (bf16[96,1536]{1,0:T(8,128)(2,1)}, bf16[96,1536]{1,0:T(8,128)(2,1)S(1)}, u32[]{:S(2)}, u32[]{:S(2)}) collective-permute-start(bf16[96,1536]{1,0:T(8,128)(2,1)} %collective-permute-done.9), channel_id=1, source_target_pairs={{0,112},{16,0},{32,16},{48,32},{64,48},{80,64},{96,80},{112,96},{1... | collective-permute-start | bytes 884744 | tf_op jit(solution)/shard_map/ppermute | solution.py:67
  90.9 7.0 %collective-permute-start.12 = (bf16[96,1536]{1,0:T(8,128)(2,1)}, bf16[96,1536]{1,0:T(8,128)(2,1)S(1)}, u32[]{:S(2)}, u32[]{:S(2)}) collective-permute-start(bf16[96,1536]{1,0:T(8,128)(2,1)} %collective-permute-done.11), channel_id=1, source_target_pairs={{0,16},{16,32},{32,48},{48,64},{64,80},{80,96},{96,112},{112,0},{1... | collective-permute-start | bytes 884744 | tf_op jit(solution)/shard_map/ppermute | solution.py:64
  97.9 7.4 %collective-permute-start.13 = (bf16[96,1536]{1,0:T(8,128)(2,1)S(1)}, bf16[96,1536]{1,0:T(8,128)(2,1)S(1)}, u32[]{:S(2)}, u32[]{:S(2)}) collective-permute-start(bf16[96,1536]{1,0:T(8,128)(2,1)S(1)} %collective-permute-done.12), channel_id=1, source_target_pairs={{0,16},{16,32},{32,48},{48,64},{64,80},{80,96},{96,112},{112,0},{1... | collective-permute-start | bytes 884744 | tf_op jit(solution)/shard_map/ppermute | solution.py:64
  110.3 46.4 %collective-permute-start.14 = (bf16[8,96,1536]{2,1,0:T(8,128)(2,1)}, bf16[8,96,1536]{2,1,0:T(8,128)(2,1)}, u32[]{:S(2)}, u32[]{:S(2)}) collective-permute-start(bf16[8,96,1536]{2,1,0:T(8,128)(2,1)} %bitcast_dynamic-update-slice_fusion), channel_id=1, source_target_pairs={{0,128},{128,0},{1,129},{129,1},{2,130},{130,2},{3,131},{131,3},{4... | collective-permute-start | bytes 7077896 | tf_op jit(solution)/shard_map/ppermute | solution.py:142
  138.0 15.2 %all-to-all-start.3 = ((bf16[16,32,192]{2,1,0:T(8,128)(2,1)}), bf16[16,32,192]{2,1,0:T(8,128)(2,1)}, u32[]{:S(2)}, u32[]{:S(2)}) async-start(bf16[16,32,192]{2,1,0:T(8,128)(2,1)} %reshape.178), calls=%async_computation.3 | async-start | bytes 524288 | tf_op jit(solution)/shard_map/all_to_all | solution.py:183
  153.2 13.5 %all-to-all-start.4 = ((bf16[8,2,32,192]{3,2,1,0:T(8,128)(2,1)}), bf16[8,2,32,192]{3,2,1,0:T(8,128)(2,1)S(1)}, u32[]{:S(2)}, u32[]{:S(2)}) async-start(bf16[8,2,32,192]{3,2,1,0:T(8,128)(2,1)} %bitcast.24), calls=%async_computation.4 | async-start | bytes 524288 | tf_op jit(solution)/shard_map/all_to_all | solution.py:184
  170.9 40.8 %copy-start.6 = (bf16[384,1536]{1,0:T(8,128)(2,1)S(1)}, bf16[384,1536]{1,0:T(8,128)(2,1)}, u32[]{:S(2)}) copy-start(bf16[384,1536]{1,0:T(8,128)(2,1)} %param.26) | copy-start | bytes 3538948
  219.2 4.6 %copy-start.5 = (f32[2,32,32]{2,1,0:T(8,128)S(1)}, f32[2,32,32]{2,1,0:T(8,128)}, u32[]{:S(2)}) copy-start(f32[2,32,32]{2,1,0:T(8,128)} %param.19) | copy-start | bytes 24580
  219.2 42.8 %all-to-all-start.6 = ((bf16[16,2,32,1536]{3,2,1,0:T(8,128)(2,1)}), bf16[16,2,32,1536]{3,2,1,0:T(8,128)(2,1)}, u32[]{:S(2)}, u32[]{:S(2)}) async-start(bf16[16,2,32,1536]{3,2,1,0:T(8,128)(2,1)} %convolution_convert_fusion), calls=%async_computation.6 | async-start | bytes 6291456 | tf_op jit(solution)/shard_map/all_to_all | solution.py:199
  223.8 47.3 %collective-permute-start.16 = (f32[2,32,32]{2,1,0:T(8,128)S(1)}, f32[2,32,32]{2,1,0:T(8,128)S(1)}, u32[]{:S(2)}, u32[]{:S(2)}) collective-permute-start(f32[2,32,32]{2,1,0:T(8,128)S(1)} %copy-done.5), channel_id=1, source_target_pairs={{0,128},{128,0},{1,129},{129,1},{2,130},{130,2},{3,131},{131,3},{4... | collective-permute-start | bytes 24584 | tf_op jit(solution)/shard_map/ppermute | solution.py:108
  227.5 37.2 %copy-start.3 = (bf16[1536,64]{0,1:T(8,128)(2,1)S(1)}, bf16[1536,64]{0,1:T(8,128)(2,1)}, u32[]{:S(2)}) copy-start(bf16[1536,64]{0,1:T(8,128)(2,1)} %param.27) | copy-start | bytes 589828
  265.0 7.0 %collective-permute-start.15 = (f32[2,32,64]{2,1,0:T(8,128)S(1)}, f32[2,32,64]{2,1,0:T(8,128)S(1)}, u32[]{:S(2)}, u32[]{:S(2)}) collective-permute-start(f32[2,32,64]{2,1,0:T(8,128)S(1)} %fusion.66), channel_id=1, source_target_pairs={{0,128},{128,0},{1,129},{129,1},{2,130},{130,2},{3,131},{131,3},{4... | collective-permute-start | bytes 49160 | tf_op jit(solution)/shard_map/ppermute | solution.py:206
  272.2 2.5 collective-permute-start.17
  274.7 4.0 %collective-permute-start.18 = (f32[2,2]{1,0:T(2,128)S(1)}, f32[2,2]{1,0:T(2,128)S(1)}, u32[]{:S(2)}, u32[]{:S(2)}) collective-permute-start(f32[2,2]{1,0:T(2,128)S(1)} %pad_maximum_fusion.4), channel_id=1, source_target_pairs={{0,2},{1,3},{2,0},{3,1},{4,6},{5,7},{6,4},{7,5},{8,10},{9,11},{10,... | collective-permute-start | bytes 56 | tf_op jit(solution)/shard_map/ppermute | solution.py:217
  278.8 2.5 collective-permute-start.19
  281.3 4.0 %collective-permute-start.20 = (f32[2,2]{1,0:T(2,128)S(1)}, f32[2,2]{1,0:T(2,128)S(1)}, u32[]{:S(2)}, u32[]{:S(2)}) collective-permute-start(f32[2,2]{1,0:T(2,128)S(1)} %pad_maximum_fusion.6), channel_id=1, source_target_pairs={{0,8},{1,9},{2,10},{3,11},{4,12},{5,13},{6,14},{7,15},{8,0},{9,1},... | collective-permute-start | bytes 56 | tf_op jit(solution)/shard_map/ppermute | solution.py:217

commit v2 on v0

--- a/solution.py
+++ b/solution.py
@@ -126,11 +126,12 @@
     activated = jax.nn.silu(pooled[0] + time_features(current)).astype(jnp.bfloat16)
     columns = jnp.dot(activated, mod_weight, preferred_element_type=jnp.float32) + mod_bias
     block_width = columns.shape[1]
-    mine = lax.all_to_all(
-        columns.reshape(req_count, group_size, block_width), "req", 0, 0, tiled=True
-    )
-    every = gather_by_a2a(mine, "seq")
-    every = every.transpose(2, 1, 0, 3).reshape(group_size, req_count * seq_count * block_width)
+    copies = jnp.broadcast_to(
+        columns.reshape(req_count, 1, group_size, block_width),
+        (req_count, seq_count, group_size, block_width),
+    ).reshape(req_count * seq_count, group_size, block_width)
+    every = lax.all_to_all(copies, ("req", "seq"), 0, 0, tiled=True)
+    every = every.transpose(1, 0, 2).reshape(group_size, req_count * seq_count * block_width)
     modulation = every.reshape(group_size, 10, 1, D)
     shift_attn, scale_attn, gate_attn = (modulation[:, 0], modulation[:, 1], modulation[:, 2])
     shift_mlp, scale_mlp, gate_mlp = (modulation[:, 3], modulation[:, 4], modulation[:, 5])
@@ -210,12 +211,9 @@
     next_latent = full_latent + step_size[:, None, None] * guided
     squares = jnp.sum(next_latent * next_latent, axis=(1, 2))
     largest = jnp.max(jnp.abs(next_latent), axis=(1, 2))
-    distance = 1
-    while distance < seq_count:
-        stats = lax.ppermute(jnp.stack([squares, largest]), "seq", xor_pairs("seq", distance))
-        squares = squares + stats[0]
-        largest = jnp.maximum(largest, stats[1])
-        distance *= 2
+    stats = gather_by_a2a(jnp.stack([squares, largest]), "seq")
+    squares = jnp.sum(stats[:, 0], axis=0)
+    largest = jnp.max(stats[:, 1], axis=0)
     guided = lax.dynamic_slice_in_dim(guided, half_index * half_values, half_values, 2)
     next_latent = lax.dynamic_slice_in_dim(next_latent, half_index * half_values, half_values, 2)
     latent_norm = jnp.sqrt(squares / (IMG * PATCHC))

time: 272 us -> 260 us (0.956); the launches traced: 269 us -> 259 us
  waiting for transfers between devices: 96.8 us -> 91.5 us
    ppermute x4 -> x0, waiting for transfers between devices: 10.7 us -> none  [on_device(): lax.ppermute(jnp.stack([squares, largest]), 'seq', xor_pairs('seq', dista...]
    all_to_all x1, starting transfers between devices: 4.07 us -> 11.4 us  [on_device(): every = lax.all_to_all(copies, ('req', 'seq'), 0, 0, tiled=True)]
    all_to_all x1, waiting for transfers between devices: 2.45 us -> 9.65 us  [on_device(): every = lax.all_to_all(copies, ('req', 'seq'), 0, 0, tiled=True)]
    all_to_all x1, waiting for transfers between devices: 0.01 us -> 4.36 us  [on_device(): own = lax.all_to_all(packed, 'seq', 0, 0, tiled=True)]
    all_to_all x1, starting transfers between devices: 6.75 us -> 3.48 us  [gather_by_a2a(): return lax.all_to_all(copies, axis, 0, 0, tiled=True)]
    all_to_all x1, waiting for transfers between devices: 30.1 us -> 27 us  [on_device(): block_terms = lax.all_to_all(mlp_terms, 'seq', 0, 0, tiled=True)]
    unnamed x47 -> x43, local copies, waits for them, and re-layouts: 15.3 us -> 13.3 us
  transfers between devices with their start and end apart: 27 -> 23, of which waited for: 16 -> 14; matrix products, arithmetic and copies ran while one was open for 19% -> 14% of each run, Pallas kernels for 0% -> 0%
where the time goes in v2:
time: 260 us; the launch traced here: 259 us
  waiting for transfers between devices  91.5 us (35%)
  starting transfers between devices  67.1 us (26%)
  blocking collectives  36.4 us (14%)
  matrix products  23.1 us (9%)
  local copies, waits for them, and re-layouts  22.4 us (9%)
  other arithmetic  17.8 us (7%)
    all_to_all x1, blocking collectives, gather_by_a2a(): return lax.all_to_all(copies, axis, 0, 0, tiled=True)  36.4 us
    all_to_all x1, waiting for transfers between devices, on_device(): block_terms = lax.all_to_all(mlp_terms, 'seq', 0, 0, tiled=True)  27 us
    ppermute x8, waiting for transfers between devices, ring_gather(): from_below = lax.ppermute(from_below, axis, up)  22 us
    unnamed x43, local copies, waits for them, and re-layouts  13.3 us
    ppermute x6, starting transfers between devices, ring_gather(): from_above = lax.ppermute(from_above, axis, down)  12.9 us
    all_to_all x1, starting transfers between devices, on_device(): every = lax.all_to_all(copies, ('req', 'seq'), 0, 0, tiled=True)  11.4 us
    ppermute x6, waiting for transfers between devices, ring_gather(): from_above = lax.ppermute(from_above, axis, down)  10.8 us
    all_to_all x1, waiting for transfers between devices, on_device(): every = lax.all_to_all(copies, ('req', 'seq'), 0, 0, tiled=True)  9.65 us
  transfers between devices with their start and end apart: 23, of which 14 were waited for; matrix products, arithmetic and copies ran while one was open for 14% of the time, Pallas kernels for 0%

profile of v2, /device:TPU:1, one launch (start us, length us, event | category | flops | bytes accessed | tf_op | source)
XLA Modules:
  0.0 259.4 jit_solution(1062873428862088950)
XLA Ops:
  0.7 1.9 bitcast_dynamic-update-slice_fusion.7
  2.5 6.4 %collective-permute-start.7 = (bf16[96,1536]{1,0:T(8,128)(2,1)S(1)}, bf16[96,1536]{1,0:T(8,128)(2,1)S(1)}, u32[]{:S(2)}, u32[]{:S(2)}) collective-permute-start(bf16[96,1536]{1,0:T(8,128)(2,1)S(1)} %get-tuple-element.15), channel_id=1, source_target_pairs={{0,112},{16,0},{32,16},{48,32},{64,48},{80,64},{96,80},{112,96},{1... | collective-permute-start | bytes 884744 | tf_op jit(solution)/shard_map/ppermute | solution.py:65
  9.9 1.2 convolution_add_fusion
  11.8 11.4 %all-to-all-start = ((f32[128,2,120]{2,1,0:T(2,128)}), f32[128,2,120]{2,1,0:T(2,128)S(1)}, u32[]{:S(2)}, u32[]{:S(2)}) async-start(f32[128,2,120]{2,1,0:T(2,128)} %bitcast.3), calls=%async_computation | async-start | bytes 262144 | tf_op jit(solution)/shard_map/all_to_all | solution.py:133
  23.2 1.0 convert_reduce_fusion.1
  24.8 9.7 %all-to-all-done = f32[128,2,120]{2,1,0:T(2,128)S(1)} async-done(((f32[128,2,120]{2,1,0:T(2,128)}), f32[128,2,120]{2,1,0:T(2,128)S(1)}, u32[]{:S(2)}, u32[]{:S(2)}) %all-to-all-start) | async-done | bytes 122912 | tf_op jit(solution)/shard_map/all_to_all | solution.py:133
  35.3 1.3 collective-permute-start.3
  36.6 1.5 collective-permute-start.8
  39.0 2.1 collective-permute-done
  41.0 1.6 collective-permute-start.1
  42.6 4.7 %collective-permute-done.8 = bf16[96,1536]{1,0:T(8,128)(2,1)S(1)} collective-permute-done((bf16[96,1536]{1,0:T(8,128)(2,1)S(1)}, bf16[96,1536]{1,0:T(8,128)(2,1)S(1)}, u32[]{:S(2)}, u32[]{:S(2)}) %collective-permute-start.8) | collective-permute-done | bytes 294944 | tf_op jit(solution)/shard_map/ppermute | solution.py:65
  47.3 1.6 collective-permute-start.9
  49.7 4.0 %collective-permute-done.1 = bf16[2,42,1536]{2,1,0:T(8,128)(2,1)S(1)} collective-permute-done((bf16[2,42,1536]{2,1,0:T(8,128)(2,1)S(1)}, bf16[2,42,1536]{2,1,0:T(8,128)(2,1)S(1)}, u32[]{:S(2)}, u32[]{:S(2)}) %collective-permute-start.1) | collective-permute-done | bytes 258080 | tf_op jit(solution)/shard_map/ppermute | solution.py:65
  53.6 1.6 collective-permute-start.2
  55.3 6.0 %collective-permute-done.12 = bf16[96,1536]{1,0:T(8,128)(2,1)S(1)} collective-permute-done((bf16[96,1536]{1,0:T(8,128)(2,1)S(1)}, bf16[96,1536]{1,0:T(8,128)(2,1)S(1)}, u32[]{:S(2)}, u32[]{:S(2)}) %collective-permute-start.12) | collective-permute-done | bytes 294944 | tf_op jit(solution)/shard_map/ppermute | solution.py:62
  62.0 5.6 %collective-permute-done.5 = bf16[2,42,1536]{2,1,0:T(8,128)(2,1)S(1)} collective-permute-done((bf16[2,42,1536]{2,1,0:T(8,128)(2,1)S(1)}, bf16[2,42,1536]{2,1,0:T(8,128)(2,1)S(1)}, u32[]{:S(2)}, u32[]{:S(2)}) %collective-permute-start.5) | collective-permute-done | bytes 258080 | tf_op jit(solution)/shard_map/ppermute | solution.py:62
  67.6 6.3 %collective-permute-done.13 = bf16[96,1536]{1,0:T(8,128)(2,1)S(1)} collective-permute-done((bf16[96,1536]{1,0:T(8,128)(2,1)S(1)}, bf16[96,1536]{1,0:T(8,128)(2,1)S(1)}, u32[]{:S(2)}, u32[]{:S(2)}) %collective-permute-start.13) | collective-permute-done | bytes 294944 | tf_op jit(solution)/shard_map/ppermute | solution.py:62
  76.1 4.1 %collective-permute-done.6 = bf16[2,42,1536]{2,1,0:T(8,128)(2,1)S(1)} collective-permute-done((bf16[2,42,1536]{2,1,0:T(8,128)(2,1)S(1)}, bf16[2,42,1536]{2,1,0:T(8,128)(2,1)S(1)}, u32[]{:S(2)}, u32[]{:S(2)}) %collective-permute-start.6) | collective-permute-done | bytes 258080 | tf_op jit(solution)/shard_map/ppermute | solution.py:62
  80.4 1.4 copy-done.6
  81.8 1.4 fusion.30
  84.0 2.1 convolution_convert_fusion.1
  86.1 3.2 %fusion.46 = bf16[16,1,22272]{2,0,1:T(8,128)(2,1)S(1)} fusion(s32[]{:T(128)S(6)} %select_n.79, bf16[16,18432]{1,0:T(8,128)(2,1)S(1)} %reshape.166, bf16[16,3840]{1,0:T(8,128)(2,1)S(1)} %bitcast.169), kind=kLoop, calls=%fused_computation.50 | loop fusion | flops 2850816 | bytes 1425412 | tf_op jit(solution)/shard_map/all_to_all | solution.py:165
  89.9 1.2 reduce.4
  91.1 1.1 reshape.183
  92.1 4.3 %all-to-all-start.1 = ((bf16[16,2,11136]{2,1,0:T(2,128)(2,1)}), bf16[16,2,11136]{2,1,0:T(2,128)(2,1)}, u32[]{:S(2)}, u32[]{:S(2)}) async-start(bf16[16,2,11136]{2,1,0:T(2,128)(2,1)} %reshape.183), calls=%async_computation.1 | async-start | bytes 1425408 | tf_op jit(solution)/shard_map/all_to_all | solution.py:165
  97.2 3.7 %collective-permute-start.14 = (bf16[8,96,1536]{2,1,0:T(8,128)(2,1)}, bf16[8,96,1536]{2,1,0:T(8,128)(2,1)}, u32[]{:S(2)}, u32[]{:S(2)}) collective-permute-start(bf16[8,96,1536]{2,1,0:T(8,128)(2,1)} %bitcast_dynamic-update-slice_fusion), channel_id=1, source_target_pairs={{0,128},{128,0},{1,129},{129,1},{2,130},{130,2},{3,131},{131,3},{4... | collective-permute-start | bytes 7077896 | tf_op jit(solution)/shard_map/ppermute | solution.py:108
  102.1 4.4 %all-to-all-done.1 = bf16[16,2,11136]{2,1,0:T(2,128)(2,1)} async-done(((bf16[16,2,11136]{2,1,0:T(2,128)(2,1)}), bf16[16,2,11136]{2,1,0:T(2,128)(2,1)}, u32[]{:S(2)}, u32[]{:S(2)}) %all-to-all-start.1) | async-done | bytes 712736 | tf_op jit(solution)/shard_map/all_to_all | solution.py:165
  106.4 4.2 %reshape.184 = bf16[16,1,22272]{2,1,0:T(2,128)(2,1)S(1)} reshape(bf16[16,2,11136]{2,1,0:T(2,128)(2,1)} %all-to-all-done.1) | data formatting | bytes 1425408
  112.2 0.8 copy.65
  113.2 4.5 %fusion.87 = (f32[3,512]{1,0:T(4,128)S(1)}, f32[3,512,672]{1,2,0:T(8,128)}) fusion(pred[672]{0:T(1024)(128)(4,1)S(1)} %iota_compare_fusion, bf16[512,3,64]{0,2,1:T(8,128)(2,1)} %bitcast.172, bf16[672,3,64]{0,2,1:T(8,128)(2,1)S(1)} %bitcast.170), kind=kOutput, calls=%fused_computation.165 | convolution fusion | flops 136250016 | bytes 4590240 | tf_op jit(solution)/shard_map/sub | solution.py:78
  117.7 2.7 %fusion.36 = bf16[512,3,64]{0,2,1:T(8,128)(2,1)S(1)} fusion(bf16[672,3,64]{0,2,1:T(8,128)(2,1)S(1)} %bitcast.171, f32[3,512,672]{1,2,0:T(8,128)} %get-tuple-element.38, f32[3,512]{1,0:T(4,128)S(1)} %get-tuple-element.37), kind=kOutput, calls=%fused_computation.41 | convolution fusion | flops 134283264 | bytes 4589568 | tf_op jit(solution)/shard_map/hqk,khd->qhd/dot_general | solution.py:80
  120.7 1.0 reshape.174
  121.7 4.2 %all-to-all-start.2 = ((bf16[16,32,192]{2,1,0:T(8,128)(2,1)}), bf16[16,32,192]{2,1,0:T(8,128)(2,1)}, u32[]{:S(2)}, u32[]{:S(2)}) async-start(bf16[16,32,192]{2,1,0:T(8,128)(2,1)} %reshape.174), calls=%async_computation.2 | async-start | bytes 524288 | tf_op jit(solution)/shard_map/all_to_all | solution.py:182
  125.9 7.5 %all-to-all-done.2 = bf16[16,32,192]{2,1,0:T(8,128)(2,1)} async-done(((bf16[16,32,192]{2,1,0:T(8,128)(2,1)}), bf16[16,32,192]{2,1,0:T(8,128)(2,1)}, u32[]{:S(2)}, u32[]{:S(2)}) %all-to-all-start.2) | async-done | bytes 196640 | tf_op jit(solution)/shard_map/all_to_all | solution.py:182
  133.4 3.8 %all-to-all-start.3 = ((bf16[8,2,32,192]{3,2,1,0:T(8,128)(2,1)}), bf16[8,2,32,192]{3,2,1,0:T(8,128)(2,1)S(1)}, u32[]{:S(2)}, u32[]{:S(2)}) async-start(bf16[8,2,32,192]{3,2,1,0:T(8,128)(2,1)} %bitcast.25), calls=%async_computation.3 | async-start | bytes 524288 | tf_op jit(solution)/shard_map/all_to_all | solution.py:183
  137.2 4.9 %broadcast_select_fusion.1 = (bf16[8,96,1536]{2,1,0:T(8,128)(2,1)}, bf16[8,96,1536]{2,1,0:T(8,128)(2,1)}) fusion(bf16[8,96,1536]{2,1,0:T(8,128)(2,1)} %bitcast_dynamic-update-slice_fusion, bf16[8,96,1536]{2,1,0:T(8,128)(2,1)} %collective-permute-done.14, pred[]{:T(512)S(6)} %eq.8), kind=kLoop, calls=%fused_computation.14 | loop fusion | flops 2359296 | bytes 9437185 | tf_op jit(solution)/shard_map/jit(_where)/select_n | solution.py:111
  142.1 4.5 %all-to-all-done.3 = bf16[8,2,32,192]{3,2,1,0:T(8,128)(2,1)S(1)} async-done(((bf16[8,2,32,192]{3,2,1,0:T(8,128)(2,1)}), bf16[8,2,32,192]{3,2,1,0:T(8,128)(2,1)S(1)}, u32[]{:S(2)}, u32[]{:S(2)}) %all-to-all-start.3) | async-done | bytes 196640 | tf_op jit(solution)/shard_map/all_to_all | solution.py:183
  146.5 3.4 %fusion.88 = (f32[2,32]{1,0:T(2,128)S(1)}, f32[2,32,1536]{2,1,0:T(8,128)S(1)}) fusion(bf16[8,96,1536]{2,1,0:T(8,128)(2,1)} %get-tuple-element.17, bf16[8,96,1536]{2,1,0:T(8,128)(2,1)} %get-tuple-element.16, s32[]{:T(128)S(6)} %select_n.83, bf16[8,2,32,192]{3,2,1,0:T(8,128)(2,1)S(1)} %all-to-all-done.3, f32[2,1536]{1,0:T(2,128)S(1)} %bitcast.177, ...), kind=kOutput, calls=%fused_computation.166 | convolution fusion | flops 311918528 | bytes 5517572 | tf_op jit(solution)/shard_map/grnk,gkd->rnd/dot_general | solution.py:187
  150.7 36.4 %all_to_all.42 = bf16[16,2,32,1536]{3,2,1,0:T(8,128)(2,1)} all-to-all(bf16[16,2,32,1536]{3,2,1,0:T(8,128)(2,1)S(1)} %broadcast_in_dim.24), channel_id=1, replica_groups=mesh['cfg'=2,'req'=8,'seq'=16] {'seq'}, dimensions={0} | all-to-all | bytes 6291456 | tf_op jit(solution)/shard_map/all_to_all | solution.py:52
  187.1 7.5 %convolution_convert_fusion = bf16[16,2,32,1536]{3,2,1,0:T(8,128)(2,1)} fusion(bf16[384,1536]{1,0:T(8,128)(2,1)S(1)} %copy-done.8, bf16[16,2,32,1536]{3,2,1,0:T(8,128)(2,1)} %all_to_all.42, bf16[1536,384]{1,0:T(8,128)(2,1)} %param.25), kind=kOutput, calls=%fused_computation.10 | convolution fusion | flops 2421030912 | bytes 8650752 | tf_op jit(solution)/shard_map/srnf,fd->srnd/dot_general | solution.py:195
  194.6 4.6 %all-to-all-start.5 = ((bf16[16,2,32,1536]{3,2,1,0:T(8,128)(2,1)}), bf16[16,2,32,1536]{3,2,1,0:T(8,128)(2,1)}, u32[]{:S(2)}, u32[]{:S(2)}) async-start(bf16[16,2,32,1536]{3,2,1,0:T(8,128)(2,1)} %convolution_convert_fusion), calls=%async_computation.5 | async-start | bytes 6291456 | tf_op jit(solution)/shard_map/all_to_all | solution.py:198
  199.2 8.1 %collective-permute-start.16 = (f32[2,32,32]{2,1,0:T(8,128)S(1)}, f32[2,32,32]{2,1,0:T(8,128)S(1)}, u32[]{:S(2)}, u32[]{:S(2)}) collective-permute-start(f32[2,32,32]{2,1,0:T(8,128)S(1)} %copy-done.7), channel_id=1, source_target_pairs={{0,128},{128,0},{1,129},{129,1},{2,130},{130,2},{3,131},{131,3},{4... | collective-permute-start | bytes 24584 | tf_op jit(solution)/shard_map/ppermute | solution.py:117
  207.5 27.0 %all-to-all-done.5 = bf16[16,2,32,1536]{3,2,1,0:T(8,128)(2,1)} async-done(((bf16[16,2,32,1536]{3,2,1,0:T(8,128)(2,1)}), bf16[16,2,32,1536]{3,2,1,0:T(8,128)(2,1)}, u32[]{:S(2)}, u32[]{:S(2)}) %all-to-all-start.5) | async-done | bytes 3145760 | tf_op jit(solution)/shard_map/all_to_all | solution.py:198
  234.4 2.4 convert_reduce_fusion
  237.5 9.4 %collective-permute-start.15 = (f32[2,32,64]{2,1,0:T(8,128)S(1)}, f32[2,32,64]{2,1,0:T(8,128)S(1)}, u32[]{:S(2)}, u32[]{:S(2)}) collective-permute-start(f32[2,32,64]{2,1,0:T(8,128)S(1)} %fusion.66), channel_id=1, source_target_pairs={{0,128},{128,0},{1,129},{129,1},{2,130},{130,2},{3,131},{131,3},{4... | collective-permute-start | bytes 49160 | tf_op jit(solution)/shard_map/ppermute | solution.py:205
  246.8 0.8 collective-permute-done.15
  248.5 3.5 %all-to-all-start.6 = ((f32[16,2,2]{2,1,0:T(2,128)}), f32[16,2,2]{2,1,0:T(2,128)S(1)}, u32[]{:S(2)}, u32[]{:S(2)}) async-start(f32[16,2,2]{2,1,0:T(2,128)} %broadcast_in_dim.25), calls=%async_computation.6 | async-start | bytes 32768 | tf_op jit(solution)/shard_map/all_to_all | solution.py:52
  253.3 5.0 %all-to-all-done.6 = f32[16,2,2]{2,1,0:T(2,128)S(1)} async-done(((f32[16,2,2]{2,1,0:T(2,128)}), f32[16,2,2]{2,1,0:T(2,128)S(1)}, u32[]{:S(2)}, u32[]{:S(2)}) %all-to-all-start.6) | async-done | bytes 288 | tf_op jit(solution)/shard_map/all_to_all | solution.py:52
  (111 shorter events, 17.8 us)
Async XLA Ops:
  0.6 79.7 %copy-start = (bf16[1536,3,192]{0,2,1:T(8,128)(2,1)S(1)}, bf16[1536,3,192]{0,2,1:T(8,128)(2,1)}, u32[]{:S(2)}) copy-start(bf16[1536,3,192]{0,2,1:T(8,128)(2,1)} %param.22) | copy-start | bytes 5308420
  0.6 23.6 %copy-start.1 = (bf16[1,2,32,1536]{3,2,1,0:T(8,128)(2,1)S(1)}, bf16[1,2,32,1536]{3,2,1,0:T(8,128)(2,1)}, u32[]{:S(2)}) copy-start(bf16[1,2,32,1536]{3,2,1,0:T(8,128)(2,1)} %param.14) | copy-start | bytes 589828
  0.7 23.8 %copy-start.2 = (bf16[1,2,10,1536]{3,1,2,0:T(2,128)(2,1)S(1)}, bf16[1,2,10,1536]{3,1,2,0:T(2,128)(2,1)}, u32[]{:S(2)}) copy-start(bf16[1,2,10,1536]{3,1,2,0:T(2,128)(2,1)} %param.15) | copy-start | bytes 184324
  2.5 34.1 %collective-permute-start.7 = (bf16[96,1536]{1,0:T(8,128)(2,1)S(1)}, bf16[96,1536]{1,0:T(8,128)(2,1)S(1)}, u32[]{:S(2)}, u32[]{:S(2)}) collective-permute-start(bf16[96,1536]{1,0:T(8,128)(2,1)S(1)} %get-tuple-element.15), channel_id=1, source_target_pairs={{0,112},{16,0},{32,16},{48,32},{64,48},{80,64},{96,80},{112,96},{1... | collective-permute-start | bytes 884744 | tf_op jit(solution)/shard_map/ppermute | solution.py:65
  8.9 29.2 %collective-permute-start.10 = (bf16[96,1536]{1,0:T(8,128)(2,1)S(1)}, bf16[96,1536]{1,0:T(8,128)(2,1)S(1)}, u32[]{:S(2)}, u32[]{:S(2)}) collective-permute-start(bf16[96,1536]{1,0:T(8,128)(2,1)S(1)} %get-tuple-element.15), channel_id=1, source_target_pairs={{0,16},{16,32},{32,48},{48,64},{64,80},{80,96},{96,112},{112,0},{1... | collective-permute-start | bytes 884744 | tf_op jit(solution)/shard_map/ppermute | solution.py:62
  11.8 22.6 %all-to-all-start = ((f32[128,2,120]{2,1,0:T(2,128)}), f32[128,2,120]{2,1,0:T(2,128)S(1)}, u32[]{:S(2)}, u32[]{:S(2)}) async-start(f32[128,2,120]{2,1,0:T(2,128)} %bitcast.3), calls=%async_computation | async-start | bytes 262144 | tf_op jit(solution)/shard_map/all_to_all | solution.py:133
  35.0 6.0 %collective-permute-start = (bf16[2,42,1536]{2,1,0:T(8,128)(2,1)S(1)}, bf16[2,42,1536]{2,1,0:T(8,128)(2,1)S(1)}, u32[]{:S(2)}, u32[]{:S(2)}) collective-permute-start(bf16[2,42,1536]{2,1,0:T(8,128)(2,1)S(1)} %pad_maximum_fusion.2), channel_id=1, source_target_pairs={{0,112},{16,0},{32,16},{48,32},{64,48},{80,64},{96,80},{112,96},{1... | collective-permute-start | bytes 774152 | tf_op jit(solution)/shard_map/ppermute | solution.py:65
  35.3 7.3 %collective-permute-start.3 = (bf16[2,42,1536]{2,1,0:T(8,128)(2,1)S(1)}, bf16[2,42,1536]{2,1,0:T(8,128)(2,1)S(1)}, u32[]{:S(2)}, u32[]{:S(2)}) collective-permute-start(bf16[2,42,1536]{2,1,0:T(8,128)(2,1)S(1)} %pad_maximum_fusion.2), channel_id=1, source_target_pairs={{0,16},{16,32},{32,48},{48,64},{64,80},{80,96},{96,112},{112,0},{1... | collective-permute-start | bytes 774152 | tf_op jit(solution)/shard_map/ppermute | solution.py:62
  36.6 10.7 %collective-permute-start.8 = (bf16[96,1536]{1,0:T(8,128)(2,1)S(1)}, bf16[96,1536]{1,0:T(8,128)(2,1)S(1)}, u32[]{:S(2)}, u32[]{:S(2)}) collective-permute-start(bf16[96,1536]{1,0:T(8,128)(2,1)S(1)} %collective-permute-done.7), channel_id=1, source_target_pairs={{0,112},{16,0},{32,16},{48,32},{64,48},{80,64},{96,80},{112,96},{1... | collective-permute-start | bytes 884744 | tf_op jit(solution)/shard_map/ppermute | solution.py:65
  38.1 37.3 %copy-start.3 = (bf16[96,1536]{1,0:T(8,128)(2,1)}, bf16[96,1536]{1,0:T(8,128)(2,1)S(1)}, u32[]{:S(2)}) copy-start(bf16[96,1536]{1,0:T(8,128)(2,1)S(1)} %collective-permute-done.10) | copy-start | bytes 884740
  38.1 10.8 %collective-permute-start.11 = (bf16[96,1536]{1,0:T(8,128)(2,1)S(1)}, bf16[96,1536]{1,0:T(8,128)(2,1)S(1)}, u32[]{:S(2)}, u32[]{:S(2)}) collective-permute-start(bf16[96,1536]{1,0:T(8,128)(2,1)S(1)} %collective-permute-done.10), channel_id=1, source_target_pairs={{0,16},{16,32},{32,48},{48,64},{64,80},{80,96},{96,112},{112,0},{1... | collective-permute-start | bytes 884744 | tf_op jit(solution)/shard_map/ppermute | solution.py:62
  41.0 12.6 %collective-permute-start.1 = (bf16[2,42,1536]{2,1,0:T(8,128)(2,1)S(1)}, bf16[2,42,1536]{2,1,0:T(8,128)(2,1)S(1)}, u32[]{:S(2)}, u32[]{:S(2)}) collective-permute-start(bf16[2,42,1536]{2,1,0:T(8,128)(2,1)S(1)} %collective-permute-done), channel_id=1, source_target_pairs={{0,112},{16,0},{32,16},{48,32},{64,48},{80,64},{96,80},{112,96},{1... | collective-permute-start | bytes 774152 | tf_op jit(solution)/shard_map/ppermute | solution.py:65
  42.6 12.6 %collective-permute-start.4 = (bf16[2,42,1536]{2,1,0:T(8,128)(2,1)S(1)}, bf16[2,42,1536]{2,1,0:T(8,128)(2,1)S(1)}, u32[]{:S(2)}, u32[]{:S(2)}) collective-permute-start(bf16[2,42,1536]{2,1,0:T(8,128)(2,1)S(1)} %collective-permute-done.3), channel_id=1, source_target_pairs={{0,16},{16,32},{32,48},{48,64},{64,80},{80,96},{96,112},{112,0},{1... | collective-permute-start | bytes 774152 | tf_op jit(solution)/shard_map/ppermute | solution.py:62
  47.3 13.9 %collective-permute-start.9 = (bf16[96,1536]{1,0:T(8,128)(2,1)S(1)}, bf16[96,1536]{1,0:T(8,128)(2,1)S(1)}, u32[]{:S(2)}, u32[]{:S(2)}) collective-permute-start(bf16[96,1536]{1,0:T(8,128)(2,1)S(1)} %collective-permute-done.8), channel_id=1, source_target_pairs={{0,112},{16,0},{32,16},{48,32},{64,48},{80,64},{96,80},{112,96},{1... | collective-permute-start | bytes 884744 | tf_op jit(solution)/shard_map/ppermute | solution.py:65
  48.9 12.4 %collective-permute-start.12 = (bf16[96,1536]{1,0:T(8,128)(2,1)S(1)}, bf16[96,1536]{1,0:T(8,128)(2,1)S(1)}, u32[]{:S(2)}, u32[]{:S(2)}) collective-permute-start(bf16[96,1536]{1,0:T(8,128)(2,1)S(1)} %collective-permute-done.11), channel_id=1, source_target_pairs={{0,16},{16,32},{32,48},{48,64},{64,80},{80,96},{96,112},{112,0},{1... | collective-permute-start | bytes 884744 | tf_op jit(solution)/shard_map/ppermute | solution.py:62
  53.6 13.9 %collective-permute-start.2 = (bf16[2,42,1536]{2,1,0:T(8,128)(2,1)S(1)}, bf16[2,42,1536]{2,1,0:T(8,128)(2,1)S(1)}, u32[]{:S(2)}, u32[]{:S(2)}) collective-permute-start(bf16[2,42,1536]{2,1,0:T(8,128)(2,1)S(1)} %collective-permute-done.1), channel_id=1, source_target_pairs={{0,112},{16,0},{32,16},{48,32},{64,48},{80,64},{96,80},{112,96},{1... | collective-permute-start | bytes 774152 | tf_op jit(solution)/shard_map/ppermute | solution.py:65
  55.2 12.4 %collective-permute-start.5 = (bf16[2,42,1536]{2,1,0:T(8,128)(2,1)S(1)}, bf16[2,42,1536]{2,1,0:T(8,128)(2,1)S(1)}, u32[]{:S(2)}, u32[]{:S(2)}) collective-permute-start(bf16[2,42,1536]{2,1,0:T(8,128)(2,1)S(1)} %collective-permute-done.4), channel_id=1, source_target_pairs={{0,16},{16,32},{32,48},{48,64},{64,80},{80,96},{96,112},{112,0},{1... | collective-permute-start | bytes 774152 | tf_op jit(solution)/shard_map/ppermute | solution.py:62
  61.3 12.6 %collective-permute-start.13 = (bf16[96,1536]{1,0:T(8,128)(2,1)S(1)}, bf16[96,1536]{1,0:T(8,128)(2,1)S(1)}, u32[]{:S(2)}, u32[]{:S(2)}) collective-permute-start(bf16[96,1536]{1,0:T(8,128)(2,1)S(1)} %collective-permute-done.12), channel_id=1, source_target_pairs={{0,16},{16,32},{32,48},{48,64},{64,80},{80,96},{96,112},{112,0},{1... | collective-permute-start | bytes 884744 | tf_op jit(solution)/shard_map/ppermute | solution.py:62
  67.6 12.6 %collective-permute-start.6 = (bf16[2,42,1536]{2,1,0:T(8,128)(2,1)S(1)}, bf16[2,42,1536]{2,1,0:T(8,128)(2,1)S(1)}, u32[]{:S(2)}, u32[]{:S(2)}) collective-permute-start(bf16[2,42,1536]{2,1,0:T(8,128)(2,1)S(1)} %collective-permute-done.5), channel_id=1, source_target_pairs={{0,16},{16,32},{32,48},{48,64},{64,80},{80,96},{96,112},{112,0},{1... | collective-permute-start | bytes 774152 | tf_op jit(solution)/shard_map/ppermute | solution.py:62
  80.3 1.4 copy-start.6
  89.9 11.0 %copy-start.9 = (s32[1,16]{1,0:T(1,128)S(1)}, s32[1,16]{1,0:T(1,128)}, u32[]{:S(2)}) copy-start(s32[1,16]{1,0:T(1,128)} %param.16) | copy-start | bytes 196
  91.0 5.4 %copy-start.4 = (bf16[96,1536]{1,0:T(8,128)(2,1)S(1)}, bf16[96,1536]{1,0:T(8,128)(2,1)}, u32[]{:S(2)}) copy-start(bf16[96,1536]{1,0:T(8,128)(2,1)} %copy-done.3) | copy-start | bytes 884740
  92.1 14.3 %all-to-all-start.1 = ((bf16[16,2,11136]{2,1,0:T(2,128)(2,1)}), bf16[16,2,11136]{2,1,0:T(2,128)(2,1)}, u32[]{:S(2)}, u32[]{:S(2)}) async-start(bf16[16,2,11136]{2,1,0:T(2,128)(2,1)} %reshape.183), calls=%async_computation.1 | async-start | bytes 1425408 | tf_op jit(solution)/shard_map/all_to_all | solution.py:165
  97.2 40.1 %collective-permute-start.14 = (bf16[8,96,1536]{2,1,0:T(8,128)(2,1)}, bf16[8,96,1536]{2,1,0:T(8,128)(2,1)}, u32[]{:S(2)}, u32[]{:S(2)}) collective-permute-start(bf16[8,96,1536]{2,1,0:T(8,128)(2,1)} %bitcast_dynamic-update-slice_fusion), channel_id=1, source_target_pairs={{0,128},{128,0},{1,129},{129,1},{2,130},{130,2},{3,131},{131,3},{4... | collective-permute-start | bytes 7077896 | tf_op jit(solution)/shard_map/ppermute | solution.py:108
  121.7 11.7 %all-to-all-start.2 = ((bf16[16,32,192]{2,1,0:T(8,128)(2,1)}), bf16[16,32,192]{2,1,0:T(8,128)(2,1)}, u32[]{:S(2)}, u32[]{:S(2)}) async-start(bf16[16,32,192]{2,1,0:T(8,128)(2,1)} %reshape.174), calls=%async_computation.2 | async-start | bytes 524288 | tf_op jit(solution)/shard_map/all_to_all | solution.py:182
  133.4 13.1 %all-to-all-start.3 = ((bf16[8,2,32,192]{3,2,1,0:T(8,128)(2,1)}), bf16[8,2,32,192]{3,2,1,0:T(8,128)(2,1)S(1)}, u32[]{:S(2)}, u32[]{:S(2)}) async-start(bf16[8,2,32,192]{3,2,1,0:T(8,128)(2,1)} %bitcast.25), calls=%async_computation.3 | async-start | bytes 524288 | tf_op jit(solution)/shard_map/all_to_all | solution.py:183
  150.7 36.4 %copy-start.8 = (bf16[384,1536]{1,0:T(8,128)(2,1)S(1)}, bf16[384,1536]{1,0:T(8,128)(2,1)}, u32[]{:S(2)}) copy-start(bf16[384,1536]{1,0:T(8,128)(2,1)} %param.26) | copy-start | bytes 3538948
  194.6 4.6 %copy-start.7 = (f32[2,32,32]{2,1,0:T(8,128)S(1)}, f32[2,32,32]{2,1,0:T(8,128)}, u32[]{:S(2)}) copy-start(f32[2,32,32]{2,1,0:T(8,128)} %param.19) | copy-start | bytes 24580
  194.6 39.8 %all-to-all-start.5 = ((bf16[16,2,32,1536]{3,2,1,0:T(8,128)(2,1)}), bf16[16,2,32,1536]{3,2,1,0:T(8,128)(2,1)}, u32[]{:S(2)}, u32[]{:S(2)}) async-start(bf16[16,2,32,1536]{3,2,1,0:T(8,128)(2,1)} %convolution_convert_fusion), calls=%async_computation.5 | async-start | bytes 6291456 | tf_op jit(solution)/shard_map/all_to_all | solution.py:198
  199.2 47.6 %collective-permute-start.16 = (f32[2,32,32]{2,1,0:T(8,128)S(1)}, f32[2,32,32]{2,1,0:T(8,128)S(1)}, u32[]{:S(2)}, u32[]{:S(2)}) collective-permute-start(f32[2,32,32]{2,1,0:T(8,128)S(1)} %copy-done.7), channel_id=1, source_target_pairs={{0,128},{128,0},{1,129},{129,1},{2,130},{130,2},{3,131},{131,3},{4... | collective-permute-start | bytes 24584 | tf_op jit(solution)/shard_map/ppermute | solution.py:117
  207.5 29.7 %copy-start.5 = (bf16[1536,64]{0,1:T(8,128)(2,1)S(1)}, bf16[1536,64]{0,1:T(8,128)(2,1)}, u32[]{:S(2)}) copy-start(bf16[1536,64]{0,1:T(8,128)(2,1)} %param.27) | copy-start | bytes 589828
  237.5 10.2 %collective-permute-start.15 = (f32[2,32,64]{2,1,0:T(8,128)S(1)}, f32[2,32,64]{2,1,0:T(8,128)S(1)}, u32[]{:S(2)}, u32[]{:S(2)}) collective-permute-start(f32[2,32,64]{2,1,0:T(8,128)S(1)} %fusion.66), channel_id=1, source_target_pairs={{0,128},{128,0},{1,129},{129,1},{2,130},{130,2},{3,131},{131,3},{4... | collective-permute-start | bytes 49160 | tf_op jit(solution)/shard_map/ppermute | solution.py:205
  248.5 9.9 %all-to-all-start.6 = ((f32[16,2,2]{2,1,0:T(2,128)}), f32[16,2,2]{2,1,0:T(2,128)S(1)}, u32[]{:S(2)}, u32[]{:S(2)}) async-start(f32[16,2,2]{2,1,0:T(2,128)} %broadcast_in_dim.25), calls=%async_computation.6 | async-start | bytes 32768 | tf_op jit(solution)/shard_map/all_to_all | solution.py:52

commit v3 on v2

--- a/solution.py
+++ b/solution.py
@@ -162,7 +162,10 @@
         [proj_img.reshape(request_count, img_size), proj_txt.reshape(request_count, -1)], axis=1
     )
     packed = jnp.roll(packed, lax.axis_index("req") * group_size, axis=0)
-    own = lax.all_to_all(packed, "seq", 0, 0, tiled=True)
+    packed_width = packed.shape[1]
+    own = lax.all_to_all(
+        packed.reshape(request_count, packed_width // 128, 128), "seq", 0, 0, tiled=True
+    ).reshape(request_count, packed_width)
     image_rows = seq_count * row_count
     text_rows = seq_count * text_block
     own_img = own[:, :img_size].reshape(image_rows, 3 * head_width)

time: 260 us -> 252 us (0.969)
  local copies, waits for them, and re-layouts: 22.4 us -> 19.2 us
    all_to_all x2 -> x0, other arithmetic: 4.39 us -> none  [on_device(): own = lax.all_to_all(packed, 'seq', 0, 0, tiled=True)]
    unnamed x43 -> x39, local copies, waits for them, and re-layouts: 13.3 us -> 9.21 us
    concatenate x0 -> x1, other arithmetic: none -> 3.2 us  [on_device(): packed = jnp.roll(packed, lax.axis_index('req') * group_size, axis=0)]
  transfers between devices with their start and end apart: 23 -> 23, of which waited for: 14 -> 14; matrix products, arithmetic and copies ran while one was open for 14% -> 13% of each run, Pallas kernels for 0% -> 0%
where the time goes in v3:
time: 252 us
  waiting for transfers between devices  89.6 us (36%)
  starting transfers between devices  66.3 us (26%)
  blocking collectives  36.4 us (14%)
  matrix products  22.2 us (9%)
  local copies, waits for them, and re-layouts  19.2 us (8%)
  other arithmetic  16.6 us (7%)
    all_to_all x1, blocking collectives, gather_by_a2a(): return lax.all_to_all(copies, axis, 0, 0, tiled=True)  36.4 us
    all_to_all x1, waiting for transfers between devices, on_device(): block_terms = lax.all_to_all(mlp_terms, 'seq', 0, 0, tiled=True)  27 us
    ppermute x8, waiting for transfers between devices, ring_gather(): from_below = lax.ppermute(from_below, axis, up)  22 us
    ppermute x6, starting transfers between devices, ring_gather(): from_above = lax.ppermute(from_above, axis, down)  12.9 us
    all_to_all x1, starting transfers between devices, on_device(): every = lax.all_to_all(copies, ('req', 'seq'), 0, 0, tiled=True)  11.4 us
    ppermute x6, waiting for transfers between devices, ring_gather(): from_above = lax.ppermute(from_above, axis, down)  9.81 us
    all_to_all x1, waiting for transfers between devices, on_device(): every = lax.all_to_all(copies, ('req', 'seq'), 0, 0, tiled=True)  9.66 us
    ppermute x1, starting transfers between devices, on_device(): other_velocity = lax.ppermute(own_velocity, 'cfg', xor_pairs('cfg', 1))  9.35 us
  transfers between devices with their start and end apart: 23, of which 14 were waited for; matrix products, arithmetic and copies ran while one was open for 13% of the time, Pallas kernels for 0%

profile of v3, /device:TPU:1, one launch (start us, length us, event | category | flops | bytes accessed | tf_op | source)
XLA Modules:
  0.0 251.5 jit_solution(2667210473081892951)
XLA Ops:
  0.7 1.9 bitcast_dynamic-update-slice_fusion.7
  2.5 6.4 %collective-permute-start.7 = (bf16[96,1536]{1,0:T(8,128)(2,1)S(1)}, bf16[96,1536]{1,0:T(8,128)(2,1)}, u32[]{:S(2)}, u32[]{:S(2)}) collective-permute-start(bf16[96,1536]{1,0:T(8,128)(2,1)S(1)} %get-tuple-element.15), channel_id=1, source_target_pairs={{0,112},{16,0},{32,16},{48,32},{64,48},{80,64},{96,80},{112,96},{1... | collective-permute-start | bytes 884744 | tf_op jit(solution)/shard_map/ppermute | solution.py:65
  9.9 1.2 convolution_add_fusion
  11.8 11.4 %all-to-all-start = ((f32[128,2,120]{2,1,0:T(2,128)}), f32[128,2,120]{2,1,0:T(2,128)S(1)}, u32[]{:S(2)}, u32[]{:S(2)}) async-start(f32[128,2,120]{2,1,0:T(2,128)} %bitcast.3), calls=%async_computation | async-start | bytes 262144 | tf_op jit(solution)/shard_map/all_to_all | solution.py:133
  23.2 1.0 convert_reduce_fusion.1
  24.8 9.7 %all-to-all-done = f32[128,2,120]{2,1,0:T(2,128)S(1)} async-done(((f32[128,2,120]{2,1,0:T(2,128)}), f32[128,2,120]{2,1,0:T(2,128)S(1)}, u32[]{:S(2)}, u32[]{:S(2)}) %all-to-all-start) | async-done | bytes 122912 | tf_op jit(solution)/shard_map/all_to_all | solution.py:133
  35.3 1.3 collective-permute-start.3
  36.6 1.5 collective-permute-start.8
  38.1 1.8 bitcast_dynamic-update-slice_fusion.6
  39.9 1.1 collective-permute-done
  41.0 1.6 collective-permute-start.1
  42.6 4.7 %collective-permute-done.8 = bf16[96,1536]{1,0:T(8,128)(2,1)S(1)} collective-permute-done((bf16[96,1536]{1,0:T(8,128)(2,1)}, bf16[96,1536]{1,0:T(8,128)(2,1)S(1)}, u32[]{:S(2)}, u32[]{:S(2)}) %collective-permute-start.8) | collective-permute-done | bytes 294944 | tf_op jit(solution)/shard_map/ppermute | solution.py:65
  47.3 1.6 collective-permute-start.9
  49.6 4.0 %collective-permute-done.1 = bf16[2,42,1536]{2,1,0:T(8,128)(2,1)S(1)} collective-permute-done((bf16[2,42,1536]{2,1,0:T(8,128)(2,1)S(1)}, bf16[2,42,1536]{2,1,0:T(8,128)(2,1)S(1)}, u32[]{:S(2)}, u32[]{:S(2)}) %collective-permute-start.1) | collective-permute-done | bytes 258080 | tf_op jit(solution)/shard_map/ppermute | solution.py:65
  53.6 1.6 collective-permute-start.2
  55.2 6.0 %collective-permute-done.12 = bf16[96,1536]{1,0:T(8,128)(2,1)S(1)} collective-permute-done((bf16[96,1536]{1,0:T(8,128)(2,1)S(1)}, bf16[96,1536]{1,0:T(8,128)(2,1)S(1)}, u32[]{:S(2)}, u32[]{:S(2)}) %collective-permute-start.12) | collective-permute-done | bytes 294944 | tf_op jit(solution)/shard_map/ppermute | solution.py:62
  62.0 5.6 %collective-permute-done.5 = bf16[2,42,1536]{2,1,0:T(8,128)(2,1)S(1)} collective-permute-done((bf16[2,42,1536]{2,1,0:T(8,128)(2,1)S(1)}, bf16[2,42,1536]{2,1,0:T(8,128)(2,1)S(1)}, u32[]{:S(2)}, u32[]{:S(2)}) %collective-permute-start.5) | collective-permute-done | bytes 258080 | tf_op jit(solution)/shard_map/ppermute | solution.py:62
  67.6 6.3 %collective-permute-done.13 = bf16[96,1536]{1,0:T(8,128)(2,1)S(1)} collective-permute-done((bf16[96,1536]{1,0:T(8,128)(2,1)S(1)}, bf16[96,1536]{1,0:T(8,128)(2,1)S(1)}, u32[]{:S(2)}, u32[]{:S(2)}) %collective-permute-start.13) | collective-permute-done | bytes 294944 | tf_op jit(solution)/shard_map/ppermute | solution.py:62
  76.1 4.1 %collective-permute-done.6 = bf16[2,42,1536]{2,1,0:T(8,128)(2,1)S(1)} collective-permute-done((bf16[2,42,1536]{2,1,0:T(8,128)(2,1)S(1)}, bf16[2,42,1536]{2,1,0:T(8,128)(2,1)S(1)}, u32[]{:S(2)}, u32[]{:S(2)}) %collective-permute-start.6) | collective-permute-done | bytes 258080 | tf_op jit(solution)/shard_map/ppermute | solution.py:62
  80.3 1.4 copy-done.5
  81.8 1.4 fusion.30
  83.2 0.8 reshape.170
  84.0 2.1 convolution_convert_fusion.1
  86.1 3.2 %fusion.45 = bf16[16,22272]{1,0:T(8,128)(2,1)S(1)} fusion(s32[]{:T(128)S(6)} %select_n.79, bf16[16,18432]{1,0:T(8,128)(2,1)S(1)} %reshape.170, bf16[16,3840]{1,0:T(8,128)(2,1)S(1)} %bitcast.169), kind=kLoop, calls=%fused_computation.49 | loop fusion | flops 2850816 | bytes 1425412 | tf_op jit(solution)/shard_map/jit(_roll_dynamic)/concatenate | solution.py:164
  89.3 1.2 reshape.173
  90.6 3.6 %all-to-all-start.1 = ((bf16[16,174,128]{2,1,0:T(8,128)(2,1)}), bf16[16,174,128]{2,1,0:T(8,128)(2,1)S(1)}, u32[]{:S(2)}, u32[]{:S(2)}) async-start(bf16[16,174,128]{2,1,0:T(8,128)(2,1)} %reshape.173), calls=%async_computation.1 | async-start | bytes 1441792 | tf_op jit(solution)/shard_map/all_to_all | solution.py:166
  94.2 1.7 bitcast_dynamic-update-slice_fusion
  95.9 3.6 %collective-permute-start.14 = (bf16[8,96,1536]{2,1,0:T(8,128)(2,1)}, bf16[8,96,1536]{2,1,0:T(8,128)(2,1)}, u32[]{:S(2)}, u32[]{:S(2)}) collective-permute-start(bf16[8,96,1536]{2,1,0:T(8,128)(2,1)} %bitcast_dynamic-update-slice_fusion), channel_id=1, source_target_pairs={{0,128},{128,0},{1,129},{129,1},{2,130},{130,2},{3,131},{131,3},{4... | collective-permute-start | bytes 7077896 | tf_op jit(solution)/shard_map/ppermute | solution.py:108
  100.8 3.4 %all-to-all-done.1 = bf16[16,174,128]{2,1,0:T(8,128)(2,1)S(1)} async-done(((bf16[16,174,128]{2,1,0:T(8,128)(2,1)}), bf16[16,174,128]{2,1,0:T(8,128)(2,1)S(1)}, u32[]{:S(2)}, u32[]{:S(2)}) %all-to-all-start.1) | async-done | bytes 712736 | tf_op jit(solution)/shard_map/all_to_all | solution.py:166
  106.2 3.6 %fusion.86 = (f32[3,512]{1,0:T(4,128)S(1)}, f32[3,512,672]{1,2,0:T(8,128)}) fusion(pred[672]{0:T(1024)(128)(4,1)S(1)} %iota_compare_fusion, bf16[512,3,64]{0,2,1:T(8,128)(2,1)S(1)} %bitcast.172, bf16[672,3,64]{0,2,1:T(8,128)(2,1)S(1)} %bitcast.170), kind=kOutput, calls=%fused_computation.164 | convolution fusion | flops 136250016 | bytes 4590240 | tf_op jit(solution)/shard_map/sub | solution.py:78
  109.8 2.7 %fusion.36 = bf16[512,3,64]{0,2,1:T(8,128)(2,1)S(1)} fusion(bf16[672,3,64]{0,2,1:T(8,128)(2,1)S(1)} %bitcast.171, f32[3,512,672]{1,2,0:T(8,128)} %get-tuple-element.38, f32[3,512]{1,0:T(4,128)S(1)} %get-tuple-element.37), kind=kOutput, calls=%fused_computation.41 | convolution fusion | flops 134283264 | bytes 4589568 | tf_op jit(solution)/shard_map/hqk,khd->qhd/dot_general | solution.py:80
  112.8 1.0 reshape.180
  113.9 4.2 %all-to-all-start.2 = ((bf16[16,32,192]{2,1,0:T(8,128)(2,1)}), bf16[16,32,192]{2,1,0:T(8,128)(2,1)}, u32[]{:S(2)}, u32[]{:S(2)}) async-start(bf16[16,32,192]{2,1,0:T(8,128)(2,1)} %reshape.180), calls=%async_computation.2 | async-start | bytes 524288 | tf_op jit(solution)/shard_map/all_to_all | solution.py:185
  118.1 7.5 %all-to-all-done.2 = bf16[16,32,192]{2,1,0:T(8,128)(2,1)} async-done(((bf16[16,32,192]{2,1,0:T(8,128)(2,1)}), bf16[16,32,192]{2,1,0:T(8,128)(2,1)}, u32[]{:S(2)}, u32[]{:S(2)}) %all-to-all-start.2) | async-done | bytes 196640 | tf_op jit(solution)/shard_map/all_to_all | solution.py:185
  125.6 3.7 %all-to-all-start.3 = ((bf16[8,2,32,192]{3,2,1,0:T(8,128)(2,1)}), bf16[8,2,32,192]{3,2,1,0:T(8,128)(2,1)S(1)}, u32[]{:S(2)}, u32[]{:S(2)}) async-start(bf16[8,2,32,192]{3,2,1,0:T(8,128)(2,1)} %bitcast.24), calls=%async_computation.3 | async-start | bytes 524288 | tf_op jit(solution)/shard_map/all_to_all | solution.py:186
  129.3 4.9 %broadcast_select_fusion.1 = (bf16[8,96,1536]{2,1,0:T(8,128)(2,1)}, bf16[8,96,1536]{2,1,0:T(8,128)(2,1)}) fusion(bf16[8,96,1536]{2,1,0:T(8,128)(2,1)} %bitcast_dynamic-update-slice_fusion, bf16[8,96,1536]{2,1,0:T(8,128)(2,1)} %collective-permute-done.14, pred[]{:T(512)S(6)} %eq.8), kind=kLoop, calls=%fused_computation.14 | loop fusion | flops 2359296 | bytes 9437185 | tf_op jit(solution)/shard_map/jit(_where)/select_n | solution.py:111
  134.2 4.4 %all-to-all-done.3 = bf16[8,2,32,192]{3,2,1,0:T(8,128)(2,1)S(1)} async-done(((bf16[8,2,32,192]{3,2,1,0:T(8,128)(2,1)}), bf16[8,2,32,192]{3,2,1,0:T(8,128)(2,1)S(1)}, u32[]{:S(2)}, u32[]{:S(2)}) %all-to-all-start.3) | async-done | bytes 196640 | tf_op jit(solution)/shard_map/all_to_all | solution.py:186
  138.7 3.4 %fusion.87 = (f32[2,32]{1,0:T(2,128)S(1)}, f32[2,32,1536]{2,1,0:T(8,128)S(1)}) fusion(bf16[8,96,1536]{2,1,0:T(8,128)(2,1)} %get-tuple-element.17, bf16[8,96,1536]{2,1,0:T(8,128)(2,1)} %get-tuple-element.16, s32[]{:T(128)S(6)} %select_n.83, bf16[8,2,32,192]{3,2,1,0:T(8,128)(2,1)S(1)} %all-to-all-done.3, f32[2,1536]{1,0:T(2,128)S(1)} %bitcast.177, ...), kind=kOutput, calls=%fused_computation.165 | convolution fusion | flops 311918528 | bytes 5517572 | tf_op jit(solution)/shard_map/grnk,gkd->rnd/dot_general | solution.py:190
  142.9 36.4 %all_to_all.35 = bf16[16,2,32,1536]{3,2,1,0:T(8,128)(2,1)} all-to-all(bf16[16,2,32,1536]{3,2,1,0:T(8,128)(2,1)S(1)} %broadcast_in_dim.24), channel_id=1, replica_groups=mesh['cfg'=2,'req'=8,'seq'=16] {'seq'}, dimensions={0} | all-to-all | bytes 6291456 | tf_op jit(solution)/shard_map/all_to_all | solution.py:52
  179.2 7.5 %convolution_convert_fusion = bf16[16,2,32,1536]{3,2,1,0:T(8,128)(2,1)} fusion(bf16[384,1536]{1,0:T(8,128)(2,1)S(1)} %copy-done.7, bf16[16,2,32,1536]{3,2,1,0:T(8,128)(2,1)} %all_to_all.35, bf16[1536,384]{1,0:T(8,128)(2,1)} %param.25), kind=kOutput, calls=%fused_computation.10 | convolution fusion | flops 2421030912 | bytes 8650752 | tf_op jit(solution)/shard_map/srnf,fd->srnd/dot_general | solution.py:198
  186.7 4.6 %all-to-all-start.5 = ((bf16[16,2,32,1536]{3,2,1,0:T(8,128)(2,1)}), bf16[16,2,32,1536]{3,2,1,0:T(8,128)(2,1)}, u32[]{:S(2)}, u32[]{:S(2)}) async-start(bf16[16,2,32,1536]{3,2,1,0:T(8,128)(2,1)} %convolution_convert_fusion), calls=%async_computation.5 | async-start | bytes 6291456 | tf_op jit(solution)/shard_map/all_to_all | solution.py:201
  191.4 8.1 %collective-permute-start.16 = (f32[2,32,32]{2,1,0:T(8,128)S(1)}, f32[2,32,32]{2,1,0:T(8,128)S(1)}, u32[]{:S(2)}, u32[]{:S(2)}) collective-permute-start(f32[2,32,32]{2,1,0:T(8,128)S(1)} %copy-done.6), channel_id=1, source_target_pairs={{0,128},{128,0},{1,129},{129,1},{2,130},{130,2},{3,131},{131,3},{4... | collective-permute-start | bytes 24584 | tf_op jit(solution)/shard_map/ppermute | solution.py:117
  199.6 27.0 %all-to-all-done.5 = bf16[16,2,32,1536]{3,2,1,0:T(8,128)(2,1)} async-done(((bf16[16,2,32,1536]{3,2,1,0:T(8,128)(2,1)}), bf16[16,2,32,1536]{3,2,1,0:T(8,128)(2,1)}, u32[]{:S(2)}, u32[]{:S(2)}) %all-to-all-start.5) | async-done | bytes 3145760 | tf_op jit(solution)/shard_map/all_to_all | solution.py:201
  226.6 2.4 convert_reduce_fusion
  229.6 9.4 %collective-permute-start.15 = (f32[2,32,64]{2,1,0:T(8,128)S(1)}, f32[2,32,64]{2,1,0:T(8,128)S(1)}, u32[]{:S(2)}, u32[]{:S(2)}) collective-permute-start(f32[2,32,64]{2,1,0:T(8,128)S(1)} %fusion.65), channel_id=1, source_target_pairs={{0,128},{128,0},{1,129},{129,1},{2,130},{130,2},{3,131},{131,3},{4... | collective-permute-start | bytes 49160 | tf_op jit(solution)/shard_map/ppermute | solution.py:208
  239.0 0.8 collective-permute-done.15
  240.6 3.5 %all-to-all-start.6 = ((f32[16,2,2]{2,1,0:T(2,128)}), f32[16,2,2]{2,1,0:T(2,128)S(1)}, u32[]{:S(2)}, u32[]{:S(2)}) async-start(f32[16,2,2]{2,1,0:T(2,128)} %broadcast_in_dim.25), calls=%async_computation.6 | async-start | bytes 32768 | tf_op jit(solution)/shard_map/all_to_all | solution.py:52
  245.5 5.0 %all-to-all-done.6 = f32[16,2,2]{2,1,0:T(2,128)S(1)} async-done(((f32[16,2,2]{2,1,0:T(2,128)}), f32[16,2,2]{2,1,0:T(2,128)S(1)}, u32[]{:S(2)}, u32[]{:S(2)}) %all-to-all-start.6) | async-done | bytes 288 | tf_op jit(solution)/shard_map/all_to_all | solution.py:52
  (106 shorter events, 15.2 us)
Async XLA Ops:
  0.6 79.7 %copy-start = (bf16[1536,3,192]{0,2,1:T(8,128)(2,1)S(1)}, bf16[1536,3,192]{0,2,1:T(8,128)(2,1)}, u32[]{:S(2)}) copy-start(bf16[1536,3,192]{0,2,1:T(8,128)(2,1)} %param.22) | copy-start | bytes 5308420
  0.6 23.6 %copy-start.1 = (bf16[1,2,32,1536]{3,2,1,0:T(8,128)(2,1)S(1)}, bf16[1,2,32,1536]{3,2,1,0:T(8,128)(2,1)}, u32[]{:S(2)}) copy-start(bf16[1,2,32,1536]{3,2,1,0:T(8,128)(2,1)} %param.14) | copy-start | bytes 589828
  0.7 23.8 %copy-start.2 = (bf16[1,2,10,1536]{3,1,2,0:T(2,128)(2,1)S(1)}, bf16[1,2,10,1536]{3,1,2,0:T(2,128)(2,1)}, u32[]{:S(2)}) copy-start(bf16[1,2,10,1536]{3,1,2,0:T(2,128)(2,1)} %param.15) | copy-start | bytes 184324
  2.5 34.1 %collective-permute-start.7 = (bf16[96,1536]{1,0:T(8,128)(2,1)S(1)}, bf16[96,1536]{1,0:T(8,128)(2,1)}, u32[]{:S(2)}, u32[]{:S(2)}) collective-permute-start(bf16[96,1536]{1,0:T(8,128)(2,1)S(1)} %get-tuple-element.15), channel_id=1, source_target_pairs={{0,112},{16,0},{32,16},{48,32},{64,48},{80,64},{96,80},{112,96},{1... | collective-permute-start | bytes 884744 | tf_op jit(solution)/shard_map/ppermute | solution.py:65
  8.9 29.2 %collective-permute-start.10 = (bf16[96,1536]{1,0:T(8,128)(2,1)S(1)}, bf16[96,1536]{1,0:T(8,128)(2,1)S(1)}, u32[]{:S(2)}, u32[]{:S(2)}) collective-permute-start(bf16[96,1536]{1,0:T(8,128)(2,1)S(1)} %get-tuple-element.15), channel_id=1, source_target_pairs={{0,16},{16,32},{32,48},{48,64},{64,80},{80,96},{96,112},{112,0},{1... | collective-permute-start | bytes 884744 | tf_op jit(solution)/shard_map/ppermute | solution.py:62
  11.8 22.6 %all-to-all-start = ((f32[128,2,120]{2,1,0:T(2,128)}), f32[128,2,120]{2,1,0:T(2,128)S(1)}, u32[]{:S(2)}, u32[]{:S(2)}) async-start(f32[128,2,120]{2,1,0:T(2,128)} %bitcast.3), calls=%async_computation | async-start | bytes 262144 | tf_op jit(solution)/shard_map/all_to_all | solution.py:133
  35.0 6.0 %collective-permute-start = (bf16[2,42,1536]{2,1,0:T(8,128)(2,1)S(1)}, bf16[2,42,1536]{2,1,0:T(8,128)(2,1)S(1)}, u32[]{:S(2)}, u32[]{:S(2)}) collective-permute-start(bf16[2,42,1536]{2,1,0:T(8,128)(2,1)S(1)} %pad_maximum_fusion.2), channel_id=1, source_target_pairs={{0,112},{16,0},{32,16},{48,32},{64,48},{80,64},{96,80},{112,96},{1... | collective-permute-start | bytes 774152 | tf_op jit(solution)/shard_map/ppermute | solution.py:65
  35.3 7.3 %collective-permute-start.3 = (bf16[2,42,1536]{2,1,0:T(8,128)(2,1)S(1)}, bf16[2,42,1536]{2,1,0:T(8,128)(2,1)S(1)}, u32[]{:S(2)}, u32[]{:S(2)}) collective-permute-start(bf16[2,42,1536]{2,1,0:T(8,128)(2,1)S(1)} %pad_maximum_fusion.2), channel_id=1, source_target_pairs={{0,16},{16,32},{32,48},{48,64},{64,80},{80,96},{96,112},{112,0},{1... | collective-permute-start | bytes 774152 | tf_op jit(solution)/shard_map/ppermute | solution.py:62
  36.6 10.7 %collective-permute-start.8 = (bf16[96,1536]{1,0:T(8,128)(2,1)}, bf16[96,1536]{1,0:T(8,128)(2,1)S(1)}, u32[]{:S(2)}, u32[]{:S(2)}) collective-permute-start(bf16[96,1536]{1,0:T(8,128)(2,1)} %collective-permute-done.7), channel_id=1, source_target_pairs={{0,112},{16,0},{32,16},{48,32},{64,48},{80,64},{96,80},{112,96},{1... | collective-permute-start | bytes 884744 | tf_op jit(solution)/shard_map/ppermute | solution.py:65
  38.1 37.3 %copy-start.3 = (bf16[96,1536]{1,0:T(8,128)(2,1)}, bf16[96,1536]{1,0:T(8,128)(2,1)S(1)}, u32[]{:S(2)}) copy-start(bf16[96,1536]{1,0:T(8,128)(2,1)S(1)} %collective-permute-done.10) | copy-start | bytes 884740
  38.1 10.8 %collective-permute-start.11 = (bf16[96,1536]{1,0:T(8,128)(2,1)S(1)}, bf16[96,1536]{1,0:T(8,128)(2,1)S(1)}, u32[]{:S(2)}, u32[]{:S(2)}) collective-permute-start(bf16[96,1536]{1,0:T(8,128)(2,1)S(1)} %collective-permute-done.10), channel_id=1, source_target_pairs={{0,16},{16,32},{32,48},{48,64},{64,80},{80,96},{96,112},{112,0},{1... | collective-permute-start | bytes 884744 | tf_op jit(solution)/shard_map/ppermute | solution.py:62
  41.0 12.6 %collective-permute-start.1 = (bf16[2,42,1536]{2,1,0:T(8,128)(2,1)S(1)}, bf16[2,42,1536]{2,1,0:T(8,128)(2,1)S(1)}, u32[]{:S(2)}, u32[]{:S(2)}) collective-permute-start(bf16[2,42,1536]{2,1,0:T(8,128)(2,1)S(1)} %collective-permute-done), channel_id=1, source_target_pairs={{0,112},{16,0},{32,16},{48,32},{64,48},{80,64},{96,80},{112,96},{1... | collective-permute-start | bytes 774152 | tf_op jit(solution)/shard_map/ppermute | solution.py:65
  42.6 12.6 %collective-permute-start.4 = (bf16[2,42,1536]{2,1,0:T(8,128)(2,1)S(1)}, bf16[2,42,1536]{2,1,0:T(8,128)(2,1)S(1)}, u32[]{:S(2)}, u32[]{:S(2)}) collective-permute-start(bf16[2,42,1536]{2,1,0:T(8,128)(2,1)S(1)} %collective-permute-done.3), channel_id=1, source_target_pairs={{0,16},{16,32},{32,48},{48,64},{64,80},{80,96},{96,112},{112,0},{1... | collective-permute-start | bytes 774152 | tf_op jit(solution)/shard_map/ppermute | solution.py:62
  47.3 13.9 %collective-permute-start.9 = (bf16[96,1536]{1,0:T(8,128)(2,1)S(1)}, bf16[96,1536]{1,0:T(8,128)(2,1)S(1)}, u32[]{:S(2)}, u32[]{:S(2)}) collective-permute-start(bf16[96,1536]{1,0:T(8,128)(2,1)S(1)} %collective-permute-done.8), channel_id=1, source_target_pairs={{0,112},{16,0},{32,16},{48,32},{64,48},{80,64},{96,80},{112,96},{1... | collective-permute-start | bytes 884744 | tf_op jit(solution)/shard_map/ppermute | solution.py:65
  48.9 12.4 %collective-permute-start.12 = (bf16[96,1536]{1,0:T(8,128)(2,1)S(1)}, bf16[96,1536]{1,0:T(8,128)(2,1)S(1)}, u32[]{:S(2)}, u32[]{:S(2)}) collective-permute-start(bf16[96,1536]{1,0:T(8,128)(2,1)S(1)} %collective-permute-done.11), channel_id=1, source_target_pairs={{0,16},{16,32},{32,48},{48,64},{64,80},{80,96},{96,112},{112,0},{1... | collective-permute-start | bytes 884744 | tf_op jit(solution)/shard_map/ppermute | solution.py:62
  53.6 13.9 %collective-permute-start.2 = (bf16[2,42,1536]{2,1,0:T(8,128)(2,1)S(1)}, bf16[2,42,1536]{2,1,0:T(8,128)(2,1)S(1)}, u32[]{:S(2)}, u32[]{:S(2)}) collective-permute-start(bf16[2,42,1536]{2,1,0:T(8,128)(2,1)S(1)} %collective-permute-done.1), channel_id=1, source_target_pairs={{0,112},{16,0},{32,16},{48,32},{64,48},{80,64},{96,80},{112,96},{1... | collective-permute-start | bytes 774152 | tf_op jit(solution)/shard_map/ppermute | solution.py:65
  55.2 12.4 %collective-permute-start.5 = (bf16[2,42,1536]{2,1,0:T(8,128)(2,1)S(1)}, bf16[2,42,1536]{2,1,0:T(8,128)(2,1)S(1)}, u32[]{:S(2)}, u32[]{:S(2)}) collective-permute-start(bf16[2,42,1536]{2,1,0:T(8,128)(2,1)S(1)} %collective-permute-done.4), channel_id=1, source_target_pairs={{0,16},{16,32},{32,48},{48,64},{64,80},{80,96},{96,112},{112,0},{1... | collective-permute-start | bytes 774152 | tf_op jit(solution)/shard_map/ppermute | solution.py:62
  61.2 12.6 %collective-permute-start.13 = (bf16[96,1536]{1,0:T(8,128)(2,1)S(1)}, bf16[96,1536]{1,0:T(8,128)(2,1)S(1)}, u32[]{:S(2)}, u32[]{:S(2)}) collective-permute-start(bf16[96,1536]{1,0:T(8,128)(2,1)S(1)} %collective-permute-done.12), channel_id=1, source_target_pairs={{0,16},{16,32},{32,48},{48,64},{64,80},{80,96},{96,112},{112,0},{1... | collective-permute-start | bytes 884744 | tf_op jit(solution)/shard_map/ppermute | solution.py:62
  67.6 12.6 %collective-permute-start.6 = (bf16[2,42,1536]{2,1,0:T(8,128)(2,1)S(1)}, bf16[2,42,1536]{2,1,0:T(8,128)(2,1)S(1)}, u32[]{:S(2)}, u32[]{:S(2)}) collective-permute-start(bf16[2,42,1536]{2,1,0:T(8,128)(2,1)S(1)} %collective-permute-done.5), channel_id=1, source_target_pairs={{0,16},{16,32},{32,48},{48,64},{64,80},{80,96},{96,112},{112,0},{1... | collective-permute-start | bytes 774152 | tf_op jit(solution)/shard_map/ppermute | solution.py:62
  80.3 1.4 copy-start.5
  86.1 13.4 %copy-start.8 = (s32[1,16]{1,0:T(1,128)S(1)}, s32[1,16]{1,0:T(1,128)}, u32[]{:S(2)}) copy-start(s32[1,16]{1,0:T(1,128)} %param.16) | copy-start | bytes 196
  90.6 13.6 %all-to-all-start.1 = ((bf16[16,174,128]{2,1,0:T(8,128)(2,1)}), bf16[16,174,128]{2,1,0:T(8,128)(2,1)S(1)}, u32[]{:S(2)}, u32[]{:S(2)}) async-start(bf16[16,174,128]{2,1,0:T(8,128)(2,1)} %reshape.173), calls=%async_computation.1 | async-start | bytes 1441792 | tf_op jit(solution)/shard_map/all_to_all | solution.py:166
  95.9 33.4 %collective-permute-start.14 = (bf16[8,96,1536]{2,1,0:T(8,128)(2,1)}, bf16[8,96,1536]{2,1,0:T(8,128)(2,1)}, u32[]{:S(2)}, u32[]{:S(2)}) collective-permute-start(bf16[8,96,1536]{2,1,0:T(8,128)(2,1)} %bitcast_dynamic-update-slice_fusion), channel_id=1, source_target_pairs={{0,128},{128,0},{1,129},{129,1},{2,130},{130,2},{3,131},{131,3},{4... | collective-permute-start | bytes 7077896 | tf_op jit(solution)/shard_map/ppermute | solution.py:108
  113.9 11.7 %all-to-all-start.2 = ((bf16[16,32,192]{2,1,0:T(8,128)(2,1)}), bf16[16,32,192]{2,1,0:T(8,128)(2,1)}, u32[]{:S(2)}, u32[]{:S(2)}) async-start(bf16[16,32,192]{2,1,0:T(8,128)(2,1)} %reshape.180), calls=%async_computation.2 | async-start | bytes 524288 | tf_op jit(solution)/shard_map/all_to_all | solution.py:185
  125.6 13.1 %all-to-all-start.3 = ((bf16[8,2,32,192]{3,2,1,0:T(8,128)(2,1)}), bf16[8,2,32,192]{3,2,1,0:T(8,128)(2,1)S(1)}, u32[]{:S(2)}, u32[]{:S(2)}) async-start(bf16[8,2,32,192]{3,2,1,0:T(8,128)(2,1)} %bitcast.24), calls=%async_computation.3 | async-start | bytes 524288 | tf_op jit(solution)/shard_map/all_to_all | solution.py:186
  142.8 36.4 %copy-start.7 = (bf16[384,1536]{1,0:T(8,128)(2,1)S(1)}, bf16[384,1536]{1,0:T(8,128)(2,1)}, u32[]{:S(2)}) copy-start(bf16[384,1536]{1,0:T(8,128)(2,1)} %param.26) | copy-start | bytes 3538948
  186.7 4.6 %copy-start.6 = (f32[2,32,32]{2,1,0:T(8,128)S(1)}, f32[2,32,32]{2,1,0:T(8,128)}, u32[]{:S(2)}) copy-start(f32[2,32,32]{2,1,0:T(8,128)} %param.19) | copy-start | bytes 24580
  186.7 39.8 %all-to-all-start.5 = ((bf16[16,2,32,1536]{3,2,1,0:T(8,128)(2,1)}), bf16[16,2,32,1536]{3,2,1,0:T(8,128)(2,1)}, u32[]{:S(2)}, u32[]{:S(2)}) async-start(bf16[16,2,32,1536]{3,2,1,0:T(8,128)(2,1)} %convolution_convert_fusion), calls=%async_computation.5 | async-start | bytes 6291456 | tf_op jit(solution)/shard_map/all_to_all | solution.py:201
  191.4 47.6 %collective-permute-start.16 = (f32[2,32,32]{2,1,0:T(8,128)S(1)}, f32[2,32,32]{2,1,0:T(8,128)S(1)}, u32[]{:S(2)}, u32[]{:S(2)}) collective-permute-start(f32[2,32,32]{2,1,0:T(8,128)S(1)} %copy-done.6), channel_id=1, source_target_pairs={{0,128},{128,0},{1,129},{129,1},{2,130},{130,2},{3,131},{131,3},{4... | collective-permute-start | bytes 24584 | tf_op jit(solution)/shard_map/ppermute | solution.py:117
  199.6 29.7 %copy-start.4 = (bf16[1536,64]{0,1:T(8,128)(2,1)S(1)}, bf16[1536,64]{0,1:T(8,128)(2,1)}, u32[]{:S(2)}) copy-start(bf16[1536,64]{0,1:T(8,128)(2,1)} %param.27) | copy-start | bytes 589828
  229.6 10.2 %collective-permute-start.15 = (f32[2,32,64]{2,1,0:T(8,128)S(1)}, f32[2,32,64]{2,1,0:T(8,128)S(1)}, u32[]{:S(2)}, u32[]{:S(2)}) collective-permute-start(f32[2,32,64]{2,1,0:T(8,128)S(1)} %fusion.65), channel_id=1, source_target_pairs={{0,128},{128,0},{1,129},{129,1},{2,130},{130,2},{3,131},{131,3},{4... | collective-permute-start | bytes 49160 | tf_op jit(solution)/shard_map/ppermute | solution.py:208
  240.6 9.8 %all-to-all-start.6 = ((f32[16,2,2]{2,1,0:T(2,128)}), f32[16,2,2]{2,1,0:T(2,128)S(1)}, u32[]{:S(2)}, u32[]{:S(2)}) async-start(f32[16,2,2]{2,1,0:T(2,128)} %broadcast_in_dim.25), calls=%async_computation.6 | async-start | bytes 32768 | tf_op jit(solution)/shard_map/all_to_all | solution.py:52

commit v4 on v3

--- a/solution.py
+++ b/solution.py
@@ -182,10 +182,16 @@
         value_rows.reshape(total_keys, local_heads, HD),
         live_keys,
     ).reshape(seq_count, row_count, head_width)
-    attended_rows = lax.all_to_all(attended, "seq", 0, 0, tiled=True)
+    attended_rows = lax.all_to_all(
+        attended.reshape(seq_count, row_count * head_width // 128, 128), "seq", 0, 0, tiled=True
+    ).reshape(seq_count, row_count, head_width)
     head_columns = lax.all_to_all(
-        attended_rows.reshape(req_count, group_size, row_count, head_width), "req", 0, 0, tiled=True
-    )
+        attended_rows.reshape(req_count, group_size * row_count * head_width // 128, 128),
+        "req",
+        0,
+        0,
+        tiled=True,
+    ).reshape(req_count, group_size, row_count, head_width)
     head_columns = jnp.roll(head_columns, -lax.axis_index("req"), axis=0)
     attn_out = jnp.einsum(
         "grnk,gkd->rnd", head_columns, every_weight, preferred_element_type=jnp.float32

time: 252 us -> 252 us (level)
  waiting for transfers between devices: 89.6 us -> 93.2 us
    all_to_all x2, waiting for transfers between devices: 12 us -> 15.8 us  [the longest x1 8.61 us: on_device(): lax.all_to_all(attended_rows.reshape(req_count, group_size * row_count *...]
    unnamed x39 -> x43, local copies, waits for them, and re-layouts: 9.21 us -> 10.2 us
  transfers between devices with their start and end apart: 23 -> 23, of which waited for: 14 -> 14; matrix products, arithmetic and copies ran while one was open for 13% -> 11% of each run, Pallas kernels for 0% -> 0%
where the time goes in v4:
time: 252 us; the launch traced here: 251 us
  waiting for transfers between devices  93.2 us (37%)
  starting transfers between devices  66.3 us (26%)
  blocking collectives  36.4 us (14%)
  matrix products  19.7 us (8%)
  local copies, waits for them, and re-layouts  19.4 us (8%)
  other arithmetic  14.5 us (6%)
    all_to_all x1, blocking collectives, gather_by_a2a(): return lax.all_to_all(copies, axis, 0, 0, tiled=True)  36.4 us
    all_to_all x1, waiting for transfers between devices, on_device(): block_terms = lax.all_to_all(mlp_terms, 'seq', 0, 0, tiled=True)  27 us
    ppermute x8, waiting for transfers between devices, ring_gather(): from_below = lax.ppermute(from_below, axis, up)  22.7 us
    ppermute x6, starting transfers between devices, ring_gather(): from_above = lax.ppermute(from_above, axis, down)  12.9 us
    all_to_all x1, starting transfers between devices, on_device(): every = lax.all_to_all(copies, ('req', 'seq'), 0, 0, tiled=True)  11.4 us
    unnamed x43, local copies, waits for them, and re-layouts  10.2 us
    ppermute x6, waiting for transfers between devices, ring_gather(): from_above = lax.ppermute(from_above, axis, down)  9.76 us
    ppermute x1, starting transfers between devices, on_device(): other_velocity = lax.ppermute(own_velocity, 'cfg', xor_pairs('cfg', 1))  9.36 us
  transfers between devices with their start and end apart: 23, of which 14 were waited for; matrix products, arithmetic and copies ran while one was open for 11% of the time, Pallas kernels for 0%

profile of v4, /device:TPU:1, one launch (start us, length us, event | category | flops | bytes accessed | tf_op | source)
XLA Modules:
  0.0 250.6 jit_solution(12911613164454714996)
XLA Ops:
  0.7 1.9 bitcast_dynamic-update-slice_fusion.7
  2.5 6.4 %collective-permute-start.7 = (bf16[96,1536]{1,0:T(8,128)(2,1)S(1)}, bf16[96,1536]{1,0:T(8,128)(2,1)}, u32[]{:S(2)}, u32[]{:S(2)}) collective-permute-start(bf16[96,1536]{1,0:T(8,128)(2,1)S(1)} %get-tuple-element.15), channel_id=1, source_target_pairs={{0,112},{16,0},{32,16},{48,32},{64,48},{80,64},{96,80},{112,96},{1... | collective-permute-start | bytes 884744 | tf_op jit(solution)/shard_map/ppermute | solution.py:65
  9.9 1.2 convolution_add_fusion
  11.8 11.4 %all-to-all-start = ((f32[128,2,120]{2,1,0:T(2,128)}), f32[128,2,120]{2,1,0:T(2,128)S(1)}, u32[]{:S(2)}, u32[]{:S(2)}) async-start(f32[128,2,120]{2,1,0:T(2,128)} %bitcast.3), calls=%async_computation | async-start | bytes 262144 | tf_op jit(solution)/shard_map/all_to_all | solution.py:133
  23.2 1.0 convert_reduce_fusion.1
  25.4 9.1 %all-to-all-done = f32[128,2,120]{2,1,0:T(2,128)S(1)} async-done(((f32[128,2,120]{2,1,0:T(2,128)}), f32[128,2,120]{2,1,0:T(2,128)S(1)}, u32[]{:S(2)}, u32[]{:S(2)}) %all-to-all-start) | async-done | bytes 122912 | tf_op jit(solution)/shard_map/all_to_all | solution.py:133
  35.3 1.3 collective-permute-start.3
  36.6 1.5 collective-permute-start.8
  38.2 1.8 bitcast_dynamic-update-slice_fusion.6
  39.9 1.1 collective-permute-done
  41.0 1.6 collective-permute-start.1
  42.6 4.7 %collective-permute-done.8 = bf16[96,1536]{1,0:T(8,128)(2,1)S(1)} collective-permute-done((bf16[96,1536]{1,0:T(8,128)(2,1)}, bf16[96,1536]{1,0:T(8,128)(2,1)S(1)}, u32[]{:S(2)}, u32[]{:S(2)}) %collective-permute-start.8) | collective-permute-done | bytes 294944 | tf_op jit(solution)/shard_map/ppermute | solution.py:65
  47.3 1.6 collective-permute-start.9
  48.9 0.8 bitcast_dynamic-update-slice_fusion.5
  49.7 3.9 %collective-permute-done.1 = bf16[2,42,1536]{2,1,0:T(8,128)(2,1)S(1)} collective-permute-done((bf16[2,42,1536]{2,1,0:T(8,128)(2,1)S(1)}, bf16[2,42,1536]{2,1,0:T(8,128)(2,1)S(1)}, u32[]{:S(2)}, u32[]{:S(2)}) %collective-permute-start.1) | collective-permute-done | bytes 258080 | tf_op jit(solution)/shard_map/ppermute | solution.py:65
  53.7 1.6 collective-permute-start.2
  55.3 6.0 %collective-permute-done.12 = bf16[96,1536]{1,0:T(8,128)(2,1)S(1)} collective-permute-done((bf16[96,1536]{1,0:T(8,128)(2,1)S(1)}, bf16[96,1536]{1,0:T(8,128)(2,1)S(1)}, u32[]{:S(2)}, u32[]{:S(2)}) %collective-permute-start.12) | collective-permute-done | bytes 294944 | tf_op jit(solution)/shard_map/ppermute | solution.py:62
  62.0 5.6 %collective-permute-done.5 = bf16[2,42,1536]{2,1,0:T(8,128)(2,1)S(1)} collective-permute-done((bf16[2,42,1536]{2,1,0:T(8,128)(2,1)S(1)}, bf16[2,42,1536]{2,1,0:T(8,128)(2,1)S(1)}, u32[]{:S(2)}, u32[]{:S(2)}) %collective-permute-start.5) | collective-permute-done | bytes 258080 | tf_op jit(solution)/shard_map/ppermute | solution.py:62
  67.6 6.3 %collective-permute-done.13 = bf16[96,1536]{1,0:T(8,128)(2,1)S(1)} collective-permute-done((bf16[96,1536]{1,0:T(8,128)(2,1)S(1)}, bf16[96,1536]{1,0:T(8,128)(2,1)S(1)}, u32[]{:S(2)}, u32[]{:S(2)}) %collective-permute-start.13) | collective-permute-done | bytes 294944 | tf_op jit(solution)/shard_map/ppermute | solution.py:62
  75.4 4.8 %collective-permute-done.6 = bf16[2,42,1536]{2,1,0:T(8,128)(2,1)S(1)} collective-permute-done((bf16[2,42,1536]{2,1,0:T(8,128)(2,1)S(1)}, bf16[2,42,1536]{2,1,0:T(8,128)(2,1)S(1)}, u32[]{:S(2)}, u32[]{:S(2)}) %collective-permute-start.6) | collective-permute-done | bytes 258080 | tf_op jit(solution)/shard_map/ppermute | solution.py:62
  80.4 1.4 copy-done.7
  81.8 1.4 fusion.30
  84.0 2.1 convolution_convert_fusion.1
  86.1 3.2 %fusion.45 = bf16[16,22272]{1,0:T(8,128)(2,1)S(1)} fusion(s32[]{:T(128)S(6)} %select_n.79, bf16[16,18432]{1,0:T(8,128)(2,1)S(1)} %reshape.167, bf16[16,3840]{1,0:T(8,128)(2,1)S(1)} %bitcast.169), kind=kLoop, calls=%fused_computation.49 | loop fusion | flops 2850816 | bytes 1425412 | tf_op jit(solution)/shard_map/jit(_roll_dynamic)/concatenate | solution.py:164
  89.3 1.2 reshape.170
  90.6 3.6 %all-to-all-start.1 = ((bf16[16,174,128]{2,1,0:T(8,128)(2,1)}), bf16[16,174,128]{2,1,0:T(8,128)(2,1)S(1)}, u32[]{:S(2)}, u32[]{:S(2)}) async-start(bf16[16,174,128]{2,1,0:T(8,128)(2,1)} %reshape.170), calls=%async_computation.1 | async-start | bytes 1441792 | tf_op jit(solution)/shard_map/all_to_all | solution.py:166
  94.2 1.7 bitcast_dynamic-update-slice_fusion.1
  96.6 3.6 %collective-permute-start.14 = (bf16[8,96,1536]{2,1,0:T(8,128)(2,1)}, bf16[8,96,1536]{2,1,0:T(8,128)(2,1)}, u32[]{:S(2)}, u32[]{:S(2)}) collective-permute-start(bf16[8,96,1536]{2,1,0:T(8,128)(2,1)} %bitcast_dynamic-update-slice_fusion), channel_id=1, source_target_pairs={{0,128},{128,0},{1,129},{129,1},{2,130},{130,2},{3,131},{131,3},{4... | collective-permute-start | bytes 7077896 | tf_op jit(solution)/shard_map/ppermute | solution.py:108
  100.9 3.3 %all-to-all-done.1 = bf16[16,174,128]{2,1,0:T(8,128)(2,1)S(1)} async-done(((bf16[16,174,128]{2,1,0:T(8,128)(2,1)}), bf16[16,174,128]{2,1,0:T(8,128)(2,1)S(1)}, u32[]{:S(2)}, u32[]{:S(2)}) %all-to-all-start.1) | async-done | bytes 712736 | tf_op jit(solution)/shard_map/all_to_all | solution.py:166
  106.2 3.5 %fusion.86 = (f32[3,512]{1,0:T(4,128)S(1)}, f32[3,512,672]{1,2,0:T(8,128)}) fusion(pred[672]{0:T(1024)(128)(4,1)S(1)} %iota_compare_fusion, bf16[512,3,64]{0,2,1:T(8,128)(2,1)S(1)} %bitcast.172, bf16[672,3,64]{0,2,1:T(8,128)(2,1)S(1)} %bitcast.170), kind=kOutput, calls=%fused_computation.164 | convolution fusion | flops 136250016 | bytes 4590240 | tf_op jit(solution)/shard_map/sub | solution.py:78
  109.7 2.7 %fusion.36 = bf16[512,3,64]{0,2,1:T(8,128)(2,1)S(1)} fusion(bf16[672,3,64]{0,2,1:T(8,128)(2,1)S(1)} %bitcast.171, f32[3,512,672]{1,2,0:T(8,128)} %get-tuple-element.38, f32[3,512]{1,0:T(4,128)S(1)} %get-tuple-element.37), kind=kOutput, calls=%fused_computation.41 | convolution fusion | flops 134283264 | bytes 4589568 | tf_op jit(solution)/shard_map/hqk,khd->qhd/dot_general | solution.py:80
  112.7 1.0 reshape_reshape.10
  113.7 4.2 %all-to-all-start.2 = ((bf16[16,48,128]{2,1,0:T(8,128)(2,1)}), bf16[16,48,128]{2,1,0:T(8,128)(2,1)}, u32[]{:S(2)}, u32[]{:S(2)}) async-start(bf16[16,48,128]{2,1,0:T(8,128)(2,1)} %reshape_reshape.10), calls=%async_computation.2 | async-start | bytes 393216 | tf_op jit(solution)/shard_map/all_to_all | solution.py:185
  117.9 7.2 %all-to-all-done.2 = bf16[16,48,128]{2,1,0:T(8,128)(2,1)} async-done(((bf16[16,48,128]{2,1,0:T(8,128)(2,1)}), bf16[16,48,128]{2,1,0:T(8,128)(2,1)}, u32[]{:S(2)}, u32[]{:S(2)}) %all-to-all-start.2) | async-done | bytes 196640 | tf_op jit(solution)/shard_map/all_to_all | solution.py:185
  125.1 3.7 %all-to-all-start.3 = ((bf16[8,96,128]{2,1,0:T(8,128)(2,1)}), bf16[8,96,128]{2,1,0:T(8,128)(2,1)S(1)}, u32[]{:S(2)}, u32[]{:S(2)}) async-start(bf16[8,96,128]{2,1,0:T(8,128)(2,1)} %bitcast.24), calls=%async_computation.3 | async-start | bytes 393216 | tf_op jit(solution)/shard_map/all_to_all | solution.py:188
  128.8 8.6 %all-to-all-done.3 = bf16[8,96,128]{2,1,0:T(8,128)(2,1)S(1)} async-done(((bf16[8,96,128]{2,1,0:T(8,128)(2,1)}), bf16[8,96,128]{2,1,0:T(8,128)(2,1)S(1)}, u32[]{:S(2)}, u32[]{:S(2)}) %all-to-all-start.3) | async-done | bytes 196640 | tf_op jit(solution)/shard_map/all_to_all | solution.py:188
  137.6 2.7 %broadcast_select_fusion.1 = (bf16[8,96,1536]{2,1,0:T(8,128)(2,1)S(1)}, bf16[8,96,1536]{2,1,0:T(8,128)(2,1)S(1)}) fusion(bf16[8,96,1536]{2,1,0:T(8,128)(2,1)} %bitcast_dynamic-update-slice_fusion, bf16[8,96,1536]{2,1,0:T(8,128)(2,1)} %collective-permute-done.14, pred[]{:T(512)S(6)} %eq.8), kind=kLoop, calls=%fused_computation.14 | loop fusion | flops 2359296 | bytes 9437185 | tf_op jit(solution)/shard_map/jit(_where)/select_n | solution.py:111
  140.3 1.1 fusion.87
  142.1 36.4 %all_to_all.35 = bf16[16,2,32,1536]{3,2,1,0:T(8,128)(2,1)} all-to-all(bf16[16,2,32,1536]{3,2,1,0:T(8,128)(2,1)S(1)} %broadcast_in_dim.24), channel_id=1, replica_groups=mesh['cfg'=2,'req'=8,'seq'=16] {'seq'}, dimensions={0} | all-to-all | bytes 6291456 | tf_op jit(solution)/shard_map/all_to_all | solution.py:52
  178.5 7.5 %convolution_convert_fusion = bf16[16,2,32,1536]{3,2,1,0:T(8,128)(2,1)} fusion(bf16[384,1536]{1,0:T(8,128)(2,1)S(1)} %copy-done.9, bf16[16,2,32,1536]{3,2,1,0:T(8,128)(2,1)} %all_to_all.35, bf16[1536,384]{1,0:T(8,128)(2,1)} %param.25), kind=kOutput, calls=%fused_computation.10 | convolution fusion | flops 2421030912 | bytes 8650752 | tf_op jit(solution)/shard_map/srnf,fd->srnd/dot_general | solution.py:204
  186.0 4.6 %all-to-all-start.5 = ((bf16[16,2,32,1536]{3,2,1,0:T(8,128)(2,1)}), bf16[16,2,32,1536]{3,2,1,0:T(8,128)(2,1)}, u32[]{:S(2)}, u32[]{:S(2)}) async-start(bf16[16,2,32,1536]{3,2,1,0:T(8,128)(2,1)} %convolution_convert_fusion), calls=%async_computation.5 | async-start | bytes 6291456 | tf_op jit(solution)/shard_map/all_to_all | solution.py:207
  190.7 8.1 %collective-permute-start.16 = (f32[2,32,32]{2,1,0:T(8,128)S(1)}, f32[2,32,32]{2,1,0:T(8,128)S(1)}, u32[]{:S(2)}, u32[]{:S(2)}) collective-permute-start(f32[2,32,32]{2,1,0:T(8,128)S(1)} %copy-done.8), channel_id=1, source_target_pairs={{0,128},{128,0},{1,129},{129,1},{2,130},{130,2},{3,131},{131,3},{4... | collective-permute-start | bytes 24584 | tf_op jit(solution)/shard_map/ppermute | solution.py:117
  198.9 27.0 %all-to-all-done.5 = bf16[16,2,32,1536]{3,2,1,0:T(8,128)(2,1)} async-done(((bf16[16,2,32,1536]{3,2,1,0:T(8,128)(2,1)}), bf16[16,2,32,1536]{3,2,1,0:T(8,128)(2,1)}, u32[]{:S(2)}, u32[]{:S(2)}) %all-to-all-start.5) | async-done | bytes 3145760 | tf_op jit(solution)/shard_map/all_to_all | solution.py:207
  225.9 2.4 convert_reduce_fusion
  228.9 9.4 %collective-permute-start.15 = (f32[2,32,64]{2,1,0:T(8,128)S(1)}, f32[2,32,64]{2,1,0:T(8,128)S(1)}, u32[]{:S(2)}, u32[]{:S(2)}) collective-permute-start(f32[2,32,64]{2,1,0:T(8,128)S(1)} %fusion.65), channel_id=1, source_target_pairs={{0,128},{128,0},{1,129},{129,1},{2,130},{130,2},{3,131},{131,3},{4... | collective-permute-start | bytes 49160 | tf_op jit(solution)/shard_map/ppermute | solution.py:214
  238.3 0.8 collective-permute-done.15
  239.9 3.4 %all-to-all-start.6 = ((f32[16,2,2]{2,1,0:T(2,128)}), f32[16,2,2]{2,1,0:T(2,128)S(1)}, u32[]{:S(2)}, u32[]{:S(2)}) async-start(f32[16,2,2]{2,1,0:T(2,128)} %broadcast_in_dim.25), calls=%async_computation.6 | async-start | bytes 32768 | tf_op jit(solution)/shard_map/all_to_all | solution.py:52
  244.7 4.8 %all-to-all-done.6 = f32[16,2,2]{2,1,0:T(2,128)S(1)} async-done(((f32[16,2,2]{2,1,0:T(2,128)}), f32[16,2,2]{2,1,0:T(2,128)S(1)}, u32[]{:S(2)}, u32[]{:S(2)}) %all-to-all-start.6) | async-done | bytes 288 | tf_op jit(solution)/shard_map/all_to_all | solution.py:52
  (111 shorter events, 15.5 us)
Async XLA Ops:
  0.6 79.7 %copy-start = (bf16[1536,3,192]{0,2,1:T(8,128)(2,1)S(1)}, bf16[1536,3,192]{0,2,1:T(8,128)(2,1)}, u32[]{:S(2)}) copy-start(bf16[1536,3,192]{0,2,1:T(8,128)(2,1)} %param.22) | copy-start | bytes 5308420
  0.6 23.6 %copy-start.1 = (bf16[1,2,32,1536]{3,2,1,0:T(8,128)(2,1)S(1)}, bf16[1,2,32,1536]{3,2,1,0:T(8,128)(2,1)}, u32[]{:S(2)}) copy-start(bf16[1,2,32,1536]{3,2,1,0:T(8,128)(2,1)} %param.14) | copy-start | bytes 589828
  0.7 23.8 %copy-start.2 = (bf16[1,2,10,1536]{3,1,2,0:T(2,128)(2,1)S(1)}, bf16[1,2,10,1536]{3,1,2,0:T(2,128)(2,1)}, u32[]{:S(2)}) copy-start(bf16[1,2,10,1536]{3,1,2,0:T(2,128)(2,1)} %param.15) | copy-start | bytes 184324
  0.7 24.1 %copy-start.10 = (s32[1,16]{1,0:T(1,128)S(1)}, s32[1,16]{1,0:T(1,128)}, u32[]{:S(2)}) copy-start(s32[1,16]{1,0:T(1,128)} %param.16) | copy-start | bytes 196
  2.5 34.1 %collective-permute-start.7 = (bf16[96,1536]{1,0:T(8,128)(2,1)S(1)}, bf16[96,1536]{1,0:T(8,128)(2,1)}, u32[]{:S(2)}, u32[]{:S(2)}) collective-permute-start(bf16[96,1536]{1,0:T(8,128)(2,1)S(1)} %get-tuple-element.15), channel_id=1, source_target_pairs={{0,112},{16,0},{32,16},{48,32},{64,48},{80,64},{96,80},{112,96},{1... | collective-permute-start | bytes 884744 | tf_op jit(solution)/shard_map/ppermute | solution.py:65
  8.9 29.2 %collective-permute-start.10 = (bf16[96,1536]{1,0:T(8,128)(2,1)S(1)}, bf16[96,1536]{1,0:T(8,128)(2,1)S(1)}, u32[]{:S(2)}, u32[]{:S(2)}) collective-permute-start(bf16[96,1536]{1,0:T(8,128)(2,1)S(1)} %get-tuple-element.15), channel_id=1, source_target_pairs={{0,16},{16,32},{32,48},{48,64},{64,80},{80,96},{96,112},{112,0},{1... | collective-permute-start | bytes 884744 | tf_op jit(solution)/shard_map/ppermute | solution.py:62
  11.8 22.6 %all-to-all-start = ((f32[128,2,120]{2,1,0:T(2,128)}), f32[128,2,120]{2,1,0:T(2,128)S(1)}, u32[]{:S(2)}, u32[]{:S(2)}) async-start(f32[128,2,120]{2,1,0:T(2,128)} %bitcast.3), calls=%async_computation | async-start | bytes 262144 | tf_op jit(solution)/shard_map/all_to_all | solution.py:133
  35.0 6.0 %collective-permute-start = (bf16[2,42,1536]{2,1,0:T(8,128)(2,1)S(1)}, bf16[2,42,1536]{2,1,0:T(8,128)(2,1)S(1)}, u32[]{:S(2)}, u32[]{:S(2)}) collective-permute-start(bf16[2,42,1536]{2,1,0:T(8,128)(2,1)S(1)} %pad_maximum_fusion.2), channel_id=1, source_target_pairs={{0,112},{16,0},{32,16},{48,32},{64,48},{80,64},{96,80},{112,96},{1... | collective-permute-start | bytes 774152 | tf_op jit(solution)/shard_map/ppermute | solution.py:65
  35.3 7.3 %collective-permute-start.3 = (bf16[2,42,1536]{2,1,0:T(8,128)(2,1)S(1)}, bf16[2,42,1536]{2,1,0:T(8,128)(2,1)S(1)}, u32[]{:S(2)}, u32[]{:S(2)}) collective-permute-start(bf16[2,42,1536]{2,1,0:T(8,128)(2,1)S(1)} %pad_maximum_fusion.2), channel_id=1, source_target_pairs={{0,16},{16,32},{32,48},{48,64},{64,80},{80,96},{96,112},{112,0},{1... | collective-permute-start | bytes 774152 | tf_op jit(solution)/shard_map/ppermute | solution.py:62
  36.6 10.7 %collective-permute-start.8 = (bf16[96,1536]{1,0:T(8,128)(2,1)}, bf16[96,1536]{1,0:T(8,128)(2,1)S(1)}, u32[]{:S(2)}, u32[]{:S(2)}) collective-permute-start(bf16[96,1536]{1,0:T(8,128)(2,1)} %collective-permute-done.7), channel_id=1, source_target_pairs={{0,112},{16,0},{32,16},{48,32},{64,48},{80,64},{96,80},{112,96},{1... | collective-permute-start | bytes 884744 | tf_op jit(solution)/shard_map/ppermute | solution.py:65
  38.1 37.3 %copy-start.3 = (bf16[96,1536]{1,0:T(8,128)(2,1)}, bf16[96,1536]{1,0:T(8,128)(2,1)S(1)}, u32[]{:S(2)}) copy-start(bf16[96,1536]{1,0:T(8,128)(2,1)S(1)} %collective-permute-done.10) | copy-start | bytes 884740
  38.1 10.8 %collective-permute-start.11 = (bf16[96,1536]{1,0:T(8,128)(2,1)S(1)}, bf16[96,1536]{1,0:T(8,128)(2,1)S(1)}, u32[]{:S(2)}, u32[]{:S(2)}) collective-permute-start(bf16[96,1536]{1,0:T(8,128)(2,1)S(1)} %collective-permute-done.10), channel_id=1, source_target_pairs={{0,16},{16,32},{32,48},{48,64},{64,80},{80,96},{96,112},{112,0},{1... | collective-permute-start | bytes 884744 | tf_op jit(solution)/shard_map/ppermute | solution.py:62
  41.0 12.6 %collective-permute-start.1 = (bf16[2,42,1536]{2,1,0:T(8,128)(2,1)S(1)}, bf16[2,42,1536]{2,1,0:T(8,128)(2,1)S(1)}, u32[]{:S(2)}, u32[]{:S(2)}) collective-permute-start(bf16[2,42,1536]{2,1,0:T(8,128)(2,1)S(1)} %collective-permute-done), channel_id=1, source_target_pairs={{0,112},{16,0},{32,16},{48,32},{64,48},{80,64},{96,80},{112,96},{1... | collective-permute-start | bytes 774152 | tf_op jit(solution)/shard_map/ppermute | solution.py:65
  42.6 12.6 %collective-permute-start.4 = (bf16[2,42,1536]{2,1,0:T(8,128)(2,1)S(1)}, bf16[2,42,1536]{2,1,0:T(8,128)(2,1)S(1)}, u32[]{:S(2)}, u32[]{:S(2)}) collective-permute-start(bf16[2,42,1536]{2,1,0:T(8,128)(2,1)S(1)} %collective-permute-done.3), channel_id=1, source_target_pairs={{0,16},{16,32},{32,48},{48,64},{64,80},{80,96},{96,112},{112,0},{1... | collective-permute-start | bytes 774152 | tf_op jit(solution)/shard_map/ppermute | solution.py:62
  47.3 13.9 %collective-permute-start.9 = (bf16[96,1536]{1,0:T(8,128)(2,1)S(1)}, bf16[96,1536]{1,0:T(8,128)(2,1)S(1)}, u32[]{:S(2)}, u32[]{:S(2)}) collective-permute-start(bf16[96,1536]{1,0:T(8,128)(2,1)S(1)} %collective-permute-done.8), channel_id=1, source_target_pairs={{0,112},{16,0},{32,16},{48,32},{64,48},{80,64},{96,80},{112,96},{1... | collective-permute-start | bytes 884744 | tf_op jit(solution)/shard_map/ppermute | solution.py:65
  48.9 31.4 %copy-start.5 = (bf16[96,1536]{1,0:T(8,128)(2,1)}, bf16[96,1536]{1,0:T(8,128)(2,1)S(1)}, u32[]{:S(2)}) copy-start(bf16[96,1536]{1,0:T(8,128)(2,1)S(1)} %collective-permute-done.11) | copy-start | bytes 884740
  48.9 12.4 %collective-permute-start.12 = (bf16[96,1536]{1,0:T(8,128)(2,1)S(1)}, bf16[96,1536]{1,0:T(8,128)(2,1)S(1)}, u32[]{:S(2)}, u32[]{:S(2)}) collective-permute-start(bf16[96,1536]{1,0:T(8,128)(2,1)S(1)} %collective-permute-done.11), channel_id=1, source_target_pairs={{0,16},{16,32},{32,48},{48,64},{64,80},{80,96},{96,112},{112,0},{1... | collective-permute-start | bytes 884744 | tf_op jit(solution)/shard_map/ppermute | solution.py:62
  53.7 13.9 %collective-permute-start.2 = (bf16[2,42,1536]{2,1,0:T(8,128)(2,1)S(1)}, bf16[2,42,1536]{2,1,0:T(8,128)(2,1)S(1)}, u32[]{:S(2)}, u32[]{:S(2)}) collective-permute-start(bf16[2,42,1536]{2,1,0:T(8,128)(2,1)S(1)} %collective-permute-done.1), channel_id=1, source_target_pairs={{0,112},{16,0},{32,16},{48,32},{64,48},{80,64},{96,80},{112,96},{1... | collective-permute-start | bytes 774152 | tf_op jit(solution)/shard_map/ppermute | solution.py:65
  55.2 12.4 %collective-permute-start.5 = (bf16[2,42,1536]{2,1,0:T(8,128)(2,1)S(1)}, bf16[2,42,1536]{2,1,0:T(8,128)(2,1)S(1)}, u32[]{:S(2)}, u32[]{:S(2)}) collective-permute-start(bf16[2,42,1536]{2,1,0:T(8,128)(2,1)S(1)} %collective-permute-done.4), channel_id=1, source_target_pairs={{0,16},{16,32},{32,48},{48,64},{64,80},{80,96},{96,112},{112,0},{1... | collective-permute-start | bytes 774152 | tf_op jit(solution)/shard_map/ppermute | solution.py:62
  61.3 12.6 %collective-permute-start.13 = (bf16[96,1536]{1,0:T(8,128)(2,1)S(1)}, bf16[96,1536]{1,0:T(8,128)(2,1)S(1)}, u32[]{:S(2)}, u32[]{:S(2)}) collective-permute-start(bf16[96,1536]{1,0:T(8,128)(2,1)S(1)} %collective-permute-done.12), channel_id=1, source_target_pairs={{0,16},{16,32},{32,48},{48,64},{64,80},{80,96},{96,112},{112,0},{1... | collective-permute-start | bytes 884744 | tf_op jit(solution)/shard_map/ppermute | solution.py:62
  67.6 12.6 %collective-permute-start.6 = (bf16[2,42,1536]{2,1,0:T(8,128)(2,1)S(1)}, bf16[2,42,1536]{2,1,0:T(8,128)(2,1)S(1)}, u32[]{:S(2)}, u32[]{:S(2)}) collective-permute-start(bf16[2,42,1536]{2,1,0:T(8,128)(2,1)S(1)} %collective-permute-done.5), channel_id=1, source_target_pairs={{0,16},{16,32},{32,48},{48,64},{64,80},{80,96},{96,112},{112,0},{1... | collective-permute-start | bytes 774152 | tf_op jit(solution)/shard_map/ppermute | solution.py:62
  80.3 1.4 copy-start.7
  89.3 6.6 %copy-start.4 = (bf16[96,1536]{1,0:T(8,128)(2,1)S(1)}, bf16[96,1536]{1,0:T(8,128)(2,1)}, u32[]{:S(2)}) copy-start(bf16[96,1536]{1,0:T(8,128)(2,1)} %copy-done.3) | copy-start | bytes 884740
  90.6 13.6 %all-to-all-start.1 = ((bf16[16,174,128]{2,1,0:T(8,128)(2,1)}), bf16[16,174,128]{2,1,0:T(8,128)(2,1)S(1)}, u32[]{:S(2)}, u32[]{:S(2)}) async-start(bf16[16,174,128]{2,1,0:T(8,128)(2,1)} %reshape.170), calls=%async_computation.1 | async-start | bytes 1441792 | tf_op jit(solution)/shard_map/all_to_all | solution.py:166
  96.6 41.0 %collective-permute-start.14 = (bf16[8,96,1536]{2,1,0:T(8,128)(2,1)}, bf16[8,96,1536]{2,1,0:T(8,128)(2,1)}, u32[]{:S(2)}, u32[]{:S(2)}) collective-permute-start(bf16[8,96,1536]{2,1,0:T(8,128)(2,1)} %bitcast_dynamic-update-slice_fusion), channel_id=1, source_target_pairs={{0,128},{128,0},{1,129},{129,1},{2,130},{130,2},{3,131},{131,3},{4... | collective-permute-start | bytes 7077896 | tf_op jit(solution)/shard_map/ppermute | solution.py:108
  113.7 11.4 %all-to-all-start.2 = ((bf16[16,48,128]{2,1,0:T(8,128)(2,1)}), bf16[16,48,128]{2,1,0:T(8,128)(2,1)}, u32[]{:S(2)}, u32[]{:S(2)}) async-start(bf16[16,48,128]{2,1,0:T(8,128)(2,1)} %reshape_reshape.10), calls=%async_computation.2 | async-start | bytes 393216 | tf_op jit(solution)/shard_map/all_to_all | solution.py:185
  125.1 12.4 %all-to-all-start.3 = ((bf16[8,96,128]{2,1,0:T(8,128)(2,1)}), bf16[8,96,128]{2,1,0:T(8,128)(2,1)S(1)}, u32[]{:S(2)}, u32[]{:S(2)}) async-start(bf16[8,96,128]{2,1,0:T(8,128)(2,1)} %bitcast.24), calls=%async_computation.3 | async-start | bytes 393216 | tf_op jit(solution)/shard_map/all_to_all | solution.py:188
  142.1 36.4 %copy-start.9 = (bf16[384,1536]{1,0:T(8,128)(2,1)S(1)}, bf16[384,1536]{1,0:T(8,128)(2,1)}, u32[]{:S(2)}) copy-start(bf16[384,1536]{1,0:T(8,128)(2,1)} %param.26) | copy-start | bytes 3538948
  186.0 4.6 %copy-start.8 = (f32[2,32,32]{2,1,0:T(8,128)S(1)}, f32[2,32,32]{2,1,0:T(8,128)}, u32[]{:S(2)}) copy-start(f32[2,32,32]{2,1,0:T(8,128)} %param.19) | copy-start | bytes 24580
  186.0 39.9 %all-to-all-start.5 = ((bf16[16,2,32,1536]{3,2,1,0:T(8,128)(2,1)}), bf16[16,2,32,1536]{3,2,1,0:T(8,128)(2,1)}, u32[]{:S(2)}, u32[]{:S(2)}) async-start(bf16[16,2,32,1536]{3,2,1,0:T(8,128)(2,1)} %convolution_convert_fusion), calls=%async_computation.5 | async-start | bytes 6291456 | tf_op jit(solution)/shard_map/all_to_all | solution.py:207
  190.7 47.6 %collective-permute-start.16 = (f32[2,32,32]{2,1,0:T(8,128)S(1)}, f32[2,32,32]{2,1,0:T(8,128)S(1)}, u32[]{:S(2)}, u32[]{:S(2)}) collective-permute-start(f32[2,32,32]{2,1,0:T(8,128)S(1)} %copy-done.8), channel_id=1, source_target_pairs={{0,128},{128,0},{1,129},{129,1},{2,130},{130,2},{3,131},{131,3},{4... | collective-permute-start | bytes 24584 | tf_op jit(solution)/shard_map/ppermute | solution.py:117
  198.9 29.7 %copy-start.6 = (bf16[1536,64]{0,1:T(8,128)(2,1)S(1)}, bf16[1536,64]{0,1:T(8,128)(2,1)}, u32[]{:S(2)}) copy-start(bf16[1536,64]{0,1:T(8,128)(2,1)} %param.27) | copy-start | bytes 589828
  228.9 10.2 %collective-permute-start.15 = (f32[2,32,64]{2,1,0:T(8,128)S(1)}, f32[2,32,64]{2,1,0:T(8,128)S(1)}, u32[]{:S(2)}, u32[]{:S(2)}) collective-permute-start(f32[2,32,64]{2,1,0:T(8,128)S(1)} %fusion.65), channel_id=1, source_target_pairs={{0,128},{128,0},{1,129},{129,1},{2,130},{130,2},{3,131},{131,3},{4... | collective-permute-start | bytes 49160 | tf_op jit(solution)/shard_map/ppermute | solution.py:214
  239.9 9.7 %all-to-all-start.6 = ((f32[16,2,2]{2,1,0:T(2,128)}), f32[16,2,2]{2,1,0:T(2,128)S(1)}, u32[]{:S(2)}, u32[]{:S(2)}) async-start(f32[16,2,2]{2,1,0:T(2,128)} %broadcast_in_dim.25), calls=%async_computation.6 | async-start | bytes 32768 | tf_op jit(solution)/shard_map/all_to_all | solution.py:52
